TPU v7x, 32 devices: a whole 2x2x4 slice. The times are simulated.
32 devices in a mesh: src: 8 (over z, core), dst: 4 (over y, x).
Axes of the slice: x: 2, y: 2, z: 4, core: 2. Of those that a mesh axis runs over, the one named last changes fastest.
Arguments:
- teleport: float32 [16, 4, 8192], P(None, 'dst', 'src'), may hold values from 0.1 to 10
- tiles: bfloat16 [4, 8, 128, 256, 256], P('dst', 'src')
- tile_rows: int32 [4, 8, 128], P('dst', 'src'), may hold values from 0 to 31
- tile_cols: int32 [4, 8, 128], P('dst', 'src'), may hold values from 0 to 15
- tile_counts: int32 [4, 8], P('dst', 'src'), may hold values from 32 to 128, as said below
- dangling: int32 [128], replicated, may hold values 0 or 1
- agg_of_block: int32 [128], replicated, may hold values from 0 to 63, as said below
- owner_list: int32 [64], replicated, may hold values from 0 to 63, each once
Outputs:
- fine_out: float32 [16, 4, 8192], P(None, 'dst', 'src')
- coarse_out: float32 [16, 64], P(None, ('src', 'dst'))
Inputs may be any that keep to these rules, and one draw needn't show every extreme that they name: `tile_counts`: slots 0 to count - 1 of a group pair's list hold its tiles, later slots are unused; some group pair fills all 128 slots. `agg_of_block`: every aggregate holds at least one block. `owner_list`: each aggregate appears once.
All inputs are finite; a program needn't handle non-finite values.
Results may differ from a plain program's by a relative error of at most 0.0003.
Values may be sent and summed in bfloat16 or wider, within the bound.
No kernel may reach another device: no remote copies, remote signals or barrier semaphores. Data moves between devices by JAX's collectives and lax.ppermute only.
A program may use at most 192 MiB of HBM per device.

v0:
```python
import jax
import jax.numpy as jnp
from jax import lax
from jax.sharding import PartitionSpec as P

damping = 0.85
group_size = 8
highest = lax.Precision.HIGHEST


def multiply(gathered, tile_set, slot_ids, col_ids, row_ids, weights, count, row_blocks):
    flat_width = gathered.shape[0] * gathered.shape[2]
    turn_count = (count + group_size - 1) // group_size

    def advance(turn, accumulated):
        first_slot = turn * group_size
        slot_pick = lax.dynamic_slice_in_dim(slot_ids, first_slot, group_size)
        col_pick = lax.dynamic_slice_in_dim(col_ids, first_slot, group_size)
        row_pick = lax.dynamic_slice_in_dim(row_ids, first_slot, group_size)
        weight_pick = lax.dynamic_slice_in_dim(weights, first_slot, group_size)
        picked = jnp.take(tile_set, slot_pick, axis=0)
        chosen = jnp.take(gathered, col_pick, axis=1) * weight_pick[None, :, None]
        product = jnp.einsum("kgj,gji->gki", chosen, picked, preferred_element_type=jnp.float32)
        return accumulated.at[row_pick].add(product.reshape(group_size, flat_width))

    return lax.fori_loop(0, turn_count, advance, jnp.zeros((row_blocks, flat_width), jnp.float32))


def per_device(
    teleport, tiles, tile_rows, tile_cols, tile_counts, dangling, agg_of_block, owner_list
):
    vectors = teleport.shape[0]
    piece_width = teleport.shape[2]
    tile_set = tiles[0, 0]
    slots_total = tile_set.shape[0]
    tile_side = tile_set.shape[2]
    blocks_piece = piece_width // tile_side
    src_count = lax.axis_size("src")
    dst_count = lax.axis_size("dst")
    row_blocks = blocks_piece * src_count
    col_blocks = blocks_piece * dst_count
    page_total = row_blocks * dst_count * tile_side
    agg_count = owner_list.shape[0]
    src_index = lax.axis_index("src")
    dst_index = lax.axis_index("dst")
    own_rows = tile_rows[0, 0]
    own_cols = tile_cols[0, 0]
    own_count = tile_counts[0, 0]
    col_global = (
        own_cols // blocks_piece * (blocks_piece * src_count)
        + src_index * blocks_piece
        + own_cols % blocks_piece
    )
    row_global = dst_index * row_blocks + own_rows
    slot_range = jnp.arange(slots_total, dtype=jnp.int32)
    live_mask = jnp.where((slot_range < own_count) & (dangling[col_global] == 0), 1, 0).astype(
        jnp.int32
    )
    piece_first = dst_index * row_blocks + src_index * blocks_piece
    piece_dangling = lax.dynamic_slice_in_dim(dangling, piece_first, blocks_piece).astype(
        jnp.float32
    )
    piece_agg = lax.dynamic_slice_in_dim(agg_of_block, piece_first, blocks_piece)
    agg_range = jnp.arange(agg_count, dtype=jnp.int32)
    piece_hot = (piece_agg[:, None] == agg_range[None, :]).astype(jnp.float32)
    tele_blocks = teleport.reshape(vectors, blocks_piece, tile_side)
    work_weights = live_mask.astype(jnp.bfloat16)

    def spread_columns(iterate):
        gathered = lax.all_gather(iterate.astype(jnp.bfloat16), "dst", axis=1, tiled=True)
        return gathered.reshape(vectors, col_blocks, tile_side)

    def relaxation(iterate):
        gathered = spread_columns(iterate)
        blocks = iterate.reshape(vectors, blocks_piece, tile_side)
        lost_sum = lax.psum(
            jnp.sum(blocks * piece_dangling[None, :, None], axis=(1, 2)), ("src", "dst")
        )
        accumulated = multiply(
            gathered, tile_set, slot_range, own_cols, own_rows, work_weights, own_count, row_blocks
        )
        own_share = lax.psum_scatter(accumulated, "src", scatter_dimension=0, tiled=True)
        image_piece = jnp.transpose(
            own_share.reshape(blocks_piece, vectors, tile_side), (1, 0, 2)
        ).reshape(iterate.shape)
        return (
            damping * (image_piece + (lost_sum / page_total)[:, None, None] * teleport)
            + (1.0 - damping) * teleport
        )

    relaxed_one = relaxation(teleport)
    relaxed_two = relaxation(relaxed_one)
    gathered = spread_columns(relaxed_two)
    blocks = relaxed_two.reshape(vectors, blocks_piece, tile_side)
    block_sums = jnp.sum(blocks, axis=2)
    tele_sums = jnp.sum(tele_blocks, axis=2)
    totals, lost_mass, weight = lax.psum(
        (
            jnp.dot(block_sums, piece_hot, precision=highest),
            jnp.dot(block_sums * piece_dangling[None, :], piece_hot, precision=highest),
            jnp.dot(tele_sums, piece_hot, precision=highest),
        ),
        ("src", "dst"),
    )
    column_sums = jnp.sum(tile_set, axis=2, dtype=jnp.float32)
    chosen = jnp.take(gathered, own_cols, axis=1) * live_mask.astype(jnp.bfloat16)[None, :, None]
    entries = jnp.einsum("ktj,tj->tk", chosen.astype(jnp.float32), column_sums, precision=highest)
    row_agg = agg_of_block[row_global]
    col_agg = agg_of_block[col_global]
    position = lax.axis_index(("src", "dst"))
    owned_count = agg_count // (src_count * dst_count)
    owned = lax.dynamic_slice_in_dim(owner_list, position * owned_count, owned_count)
    col_hot = (col_agg[:, None] == agg_range[None, :]).astype(jnp.float32)
    owner_hot = (row_agg[:, None] == owner_list[None, :]).astype(jnp.float32)
    spread_entries = (entries[:, :, None] * col_hot[:, None, :]).reshape(
        slots_total, vectors * agg_count
    )
    partial_value = lax.dot_general(
        owner_hot, spread_entries, (((0,), (0,)), ((), ())), precision=highest
    )
    coupling = lax.psum_scatter(
        partial_value, ("src", "dst"), scatter_dimension=0, tiled=True
    ).reshape(owned_count, vectors, agg_count)
    owned_hot = (owned[:, None] == agg_range[None, :]).astype(jnp.float32)
    own_weight = lax.dot_general(weight, owned_hot, (((1,), (1,)), ((), ())), precision=highest)
    order_hot = (owner_list[:, None] == agg_range[None, :]).astype(jnp.float32)

    def coarse_sweep(ratios):
        inflow = jnp.einsum("qkb,kb->kq", coupling, ratios, precision=highest)
        carried = jnp.sum(lost_mass * ratios, axis=1)
        return (
            damping * (inflow + (carried / page_total)[:, None] * own_weight)
            + (1.0 - damping) * own_weight
        )

    def collect(level_in):
        everyone = lax.all_gather(level_in, ("src", "dst"), axis=1, tiled=True)
        return jnp.dot(everyone, order_hot, precision=highest) / totals

    level_one = coarse_sweep(jnp.ones((vectors, agg_count), jnp.float32))
    level_two = coarse_sweep(collect(level_one))
    ratios = collect(level_two)
    rescale = lax.dot_general(ratios, piece_hot, (((1,), (1,)), ((), ())), precision=highest)
    corrected = (blocks * rescale[:, :, None]).reshape(relaxed_two.shape)
    corrected, coarse_out = (corrected, level_two)
    relaxed_three = relaxation(corrected)
    return (relaxation(relaxed_three), coarse_out)


def solution(mesh):
    placed = (
        P(None, "dst", "src"),
        P("dst", "src", None, None, None),
        P("dst", "src", None),
        P("dst", "src", None),
        P("dst", "src"),
        P(),
        P(),
        P(),
    )
    return jax.shard_map(
        per_device,
        mesh=mesh,
        in_specs=placed,
        out_specs=(P(None, "dst", "src"), P(None, ("src", "dst"))),
        check_vma=False,
    )
```

profile of v0, /device:TPU:0, one launch (start us, length us, event | category | flops | bytes accessed | tf_op | source)
XLA Modules:
  0.0 1115.4 jit_solution(9291008309510260702)
XLA Ops:
  8.7 9.9 all_gather.21
  21.3 79.6 %while.40 = (s32[]{:T(128)}, f32[32,4096]{1,0:T(8,128)S(1)}, s32[]{:T(128)}, s32[128]{0:T(128)}, s32[128]{0:T(128)}, /*index=5*/bf16[16,16,256]{2,0,1:T(8,128)(2...) while((s32[]{:T(128)}, f32[32,4096]{1,0:T(8,128)S(1)}, ...), condition=%wide.region_2.5_spmd, body=%wide.region_0.4_spmd.sunk | while | flops 17401980 | bytes 4137575 | solution.py:26
  22.0 6.4 gather_fusion
  32.0 6.4 gather_fusion
  41.9 6.4 gather_fusion
  51.9 6.4 gather_fusion
  61.8 6.4 gather_fusion
  71.8 6.4 gather_fusion
  81.7 6.4 gather_fusion
  91.6 6.4 gather_fusion
  101.7 7.6 convert_reduce_fusion
  109.7 119.2 %psum.49 = f32[16]{0:T(128)S(1)} all-reduce(f32[16]{0:T(128)S(1)} %multiply_reduce_fusion.3), channel_id=1, replica_groups=mesh['src'=8,'dst'=4] {'src','dst'}, use_global_device_ids=true, to_apply=%region_5.8 | all-reduce | flops 16 | bytes 128 | tf_op jit(solution)/shard_map/psum | solution.py:76
  239.1 8.4 all_gather.22
  247.8 69.1 %while.41 = (s32[]{:T(128)}, f32[32,4096]{1,0:T(8,128)S(1)}, s32[]{:T(128)}, s32[128]{0:T(128)S(1)}, s32[128]{0:T(128)S(1)}, /*index=5*/bf16[16,16,256]{2,0,1:T(...) while((s32[]{:T(128)}, f32[32,4096]{1,0:T(8,128)S(1)}, ...), condition=%wide.region_8.11_spmd, body=%wide.region_6.10_spmd.sunk | while | flops 17401980 | bytes 4137575 | solution.py:26
  248.0 6.4 gather_fusion.2
  256.6 6.4 gather_fusion.2
  265.2 6.4 gather_fusion.2
  319.1 107.5 %psum.50 = f32[16]{0:T(128)S(1)} all-reduce(f32[16]{0:T(128)S(1)} %get-tuple-element.415), channel_id=1, replica_groups=mesh['src'=8,'dst'=4] {'src','dst'}, use_global_device_ids=true, to_apply=%region_11.14 | all-reduce | flops 16 | bytes 128 | tf_op jit(solution)/shard_map/psum | solution.py:76
  426.6 14.9 %all-reduce.14.cloned.1.call-done = f32[32,4096]{1,0:T(8,128)} async-done(((f32[32,4096]{1,0:T(8,128)}), f32[32,4096]{1,0:T(8,128)}) %all-reduce.14.cloned.1.call-update) | async-done | bytes 524304
  443.1 8.4 all_gather.23
  454.9 38.9 %all-reduce.5 = (f32[16,64]{1,0:T(8,128)S(1)}, f32[16,64]{1,0:T(8,128)S(1)}, f32[16,64]{1,0:T(8,128)S(1)}) all-reduce(f32[16,64]{1,0:T(8,128)S(1)} %fusion.54, f32[16,64]{1,0:T(8,128)S(1)} %fusion.55, f32[16,64]{1,0:T(8,128)S(1)} %fusion.50), channel_id=1, replica_groups=mesh['src'=8,'dst'=4] {'src','dst'}, use_global_device_ids=true, to_apply=%region_19.22 | all-reduce | flops 3072 | bytes 24576 | tf_op jit(solution)/shard_map/psum | solution.py:97
  494.1 84.0 %all-reduce.16.cloned.1.call-done = f32[64,1024]{1,0:T(8,128)} async-done(((f32[64,1024]{1,0:T(8,128)}), f32[64,1024]{1,0:T(8,128)}) %all-reduce.16.cloned.1.call-update) | async-done | bytes 262160
  579.3 65.3 %all-gather = f32[32,2,16]{2,1,0:T(2,128)S(1)} all-gather(f32[1,2,16]{2,1,0:T(2,128)S(1)} %fusion.62), channel_id=1, replica_groups=mesh['src'=8,'dst'=4] {'src','dst'}, dimensions={0}, use_global_device_ids=true | all-gather | bytes 4224 | tf_op jit(solution)/shard_map/all_gather | solution.py:137
  645.3 63.8 %all-gather.1 = f32[32,2,16]{2,1,0:T(2,128)S(1)} all-gather(f32[1,2,16]{2,1,0:T(2,128)S(1)} %bitcast.167), channel_id=1, replica_groups=mesh['src'=8,'dst'=4] {'src','dst'}, dimensions={0}, use_global_device_ids=true | all-gather | bytes 4224 | tf_op jit(solution)/shard_map/all_gather | solution.py:137
  709.7 8.8 all_gather.26
  718.9 69.1 %while.42 = (s32[]{:T(128)}, f32[32,4096]{1,0:T(8,128)S(1)}, s32[]{:T(128)}, s32[128]{0:T(128)S(1)}, s32[128]{0:T(128)S(1)}, /*index=5*/bf16[16,16,256]{2,0,1:T(...) while((s32[]{:T(128)}, f32[32,4096]{1,0:T(8,128)S(1)}, ...), condition=%wide.region_23.26_spmd, body=%wide.region_21.25_spmd.sunk | while | flops 17401980 | bytes 4137575 | solution.py:26
  789.0 97.7 %psum.54 = f32[16]{0:T(128)S(1)} all-reduce(f32[16]{0:T(128)S(1)} %get-tuple-element.417), channel_id=1, replica_groups=mesh['src'=8,'dst'=4] {'src','dst'}, use_global_device_ids=true, to_apply=%region_26.29 | all-reduce | flops 16 | bytes 128 | tf_op jit(solution)/shard_map/psum | solution.py:76
  886.8 17.0 %all-reduce.18.cloned.1.call-done = f32[32,4096]{1,0:T(8,128)} async-done(((f32[32,4096]{1,0:T(8,128)}), f32[32,4096]{1,0:T(8,128)}) %all-reduce.18.cloned.1.call-update) | async-done | bytes 524304
  904.9 8.4 all_gather.27
  913.7 69.1 %while.43 = (s32[]{:T(128)}, f32[32,4096]{1,0:T(8,128)S(1)}, s32[]{:T(128)}, s32[128]{0:T(128)S(1)}, s32[128]{0:T(128)S(1)}, /*index=5*/bf16[16,16,256]{2,0,1:T(...) while((s32[]{:T(128)}, f32[32,4096]{1,0:T(8,128)S(1)}, ...), condition=%wide.region_29.32_spmd, body=%wide.region_27.31_spmd.sunk | while | flops 17401980 | bytes 4137575 | solution.py:26
  983.6 107.7 %psum.55 = f32[16]{0:T(128)S(1)} all-reduce(f32[16]{0:T(128)S(1)} %get-tuple-element.413), channel_id=1, replica_groups=mesh['src'=8,'dst'=4] {'src','dst'}, use_global_device_ids=true, to_apply=%region_32.35 | all-reduce | flops 16 | bytes 128 | tf_op jit(solution)/shard_map/psum | solution.py:76
  1091.3 15.8 %all-reduce.20.cloned.1.call-done = f32[32,4096]{1,0:T(8,128)} async-done(((f32[32,4096]{1,0:T(8,128)}), f32[32,4096]{1,0:T(8,128)}) %all-reduce.20.cloned.1.call-update) | async-done | bytes 524304
  (436 shorter events, 243.9 us)
Async XLA Ops:
  7.2 230.7 %all-reduce.12.cloned.1.call-start = ((), (), s32[]{:S(2)}) async-start(), calls=%async_computation | async-start | bytes 1048576
  100.8 0.8 copy-start.3
  100.8 8.5 copy-start.7
  100.9 8.5 copy-start.10
  100.9 8.5 copy-start.1
  100.9 8.7 copy-start.6
  100.9 127.9 %copy-start = (s32[128]{0:T(128)S(1)}, s32[128]{0:T(128)}, u32[]{:S(2)}) copy-start(s32[128]{0:T(128)} %param.26) | copy-start | bytes 1540
  100.9 129.7 %copy-start.11 = (u32[32]{0:T(128)S(1)}, u32[32]{0:T(128)}, u32[]{:S(2)}) copy-start(u32[32]{0:T(128)} %constant.174) | copy-start | bytes 388
  101.7 339.8 %all-reduce.14.cloned.1.call-start = ((), (), s32[]{:S(2)}) async-start(), calls=%async_computation.1 | async-start | bytes 1048576
  247.8 71.2 %copy-start.9 = (s32[64]{0:T(128)S(1)}, s32[64]{0:T(128)}, u32[]{:S(2)}) copy-start(s32[64]{0:T(128)} %param.27) | copy-start | bytes 772
  316.9 0.8 copy-start.4
  317.7 260.4 %all-reduce.16.cloned.1.call-start = ((), (), s32[]{:S(2)}) async-start(), calls=%async_computation.2 | async-start | bytes 524288
  454.8 448.9 %all-reduce.18.cloned.1.call-start = ((), (), s32[]{:S(2)}) async-start(), calls=%async_computation.3 | async-start | bytes 1048576
  645.3 73.6 %copy-start.8 = (f32[16,2]{0,1:T(2,128)}, f32[16,2]{0,1:T(2,128)S(1)}, u32[]{:S(2)}) copy-start(f32[16,2]{0,1:T(2,128)S(1)} %fusion.59) | copy-start | bytes 388
  788.0 0.8 copy-start.5
  788.8 318.3 %all-reduce.20.cloned.1.call-start = ((), (), s32[]{:S(2)}) async-start(), calls=%async_computation.4 | async-start | bytes 1048576
  982.7 0.8 copy-start.2
Sparse Core Ops, SparseCore 0:
  101.8 136.0 all-reduce.11
  317.9 123.5 all-reduce.13
  454.9 123.1 all-reduce.15
  788.9 114.7 all-reduce.17
  983.7 123.3 all-reduce.19
where the time goes:
time: 1120 us
  blocking collectives  644 us (58%)
  local copies, waits for them, and re-layouts  244 us (22%)
  waiting for transfers between devices  138 us (12%)
  other arithmetic  56.9 us (5%)
  between operations  15.7 us (1%)
  matrix products  14.4 us (1%)
    psum x4, blocking collectives, relaxation(): lax.psum(jnp.sum(blocks * piece_dangling[None, :, None], axis=(1, 2)), ('...  432 us
    gather x32, local copies, waits for them, and re-layouts, advance(): picked = jnp.take(tile_set, slot_pick, axis=0)  204 us
    unnamed x10, waiting for transfers between devices  138 us
    all_gather x2, blocking collectives, collect(): everyone = lax.all_gather(level_in, ('src', 'dst'), axis=1, tiled=True)  129 us
    all_gather x5, blocking collectives, spread_columns(): lax.all_gather(iterate.astype(jnp.bfloat16), 'dst', axis=1, tiled=True)  44.1 us
    psum x1, blocking collectives, per_device(): lax.psum((jnp.dot(block_sums, piece_hot, precision=highest), jnp.dot(bloc...  38.9 us
    scatter-add x32, other arithmetic, advance(): return accumulated.at[row_pick].add(product.reshape(group_size, flat_width))  31 us
  transfers between devices with their start and end apart: 5, of which 5 were waited for; matrix products, arithmetic and copies ran while one was open for 1% of the time, Pallas kernels for 0%

commit v1 on v0

v1 whole, which is shorter than its diff:
```python
import functools

import jax
import jax.numpy as jnp
from jax import lax
from jax.experimental import pallas as pl
from jax.experimental.pallas import tpu as pltpu
from jax.sharding import PartitionSpec as P

damping = 0.85
group_size = 8
highest = lax.Precision.HIGHEST


def tile_kernel(mode, rows_ref, cols_ref, live_ref, nb_ref, x_ref, t_ref, o_ref):
    step = pl.program_id(0)
    if mode == "image":

        @pl.when(step == 0)
        def _():
            o_ref[...] = jnp.zeros_like(o_ref)

    for g in range(group_size):
        slot = step * group_size + g
        live = live_ref[slot] != 0

        @pl.when(live)
        def _():
            product = jnp.dot(
                x_ref[cols_ref[slot]], t_ref[g], preferred_element_type=jnp.float32
            )
            if mode == "image":
                row = rows_ref[slot]
                o_ref[row] = o_ref[row] + product
            else:
                row_sum = jnp.sum(product, axis=1, keepdims=True)
                o_ref[g] = jnp.broadcast_to(row_sum, o_ref.shape[1:])

        if mode == "entries":

            @pl.when(jnp.logical_not(live))
            def _():
                o_ref[g] = jnp.zeros(o_ref.shape[1:], o_ref.dtype)


def tile_pass(mode, x_cols, tiles, rows, cols, live, block_count, row_blocks):
    col_blocks, vectors, side = x_cols.shape
    slots = tiles.shape[2]
    steps = slots // group_size

    def tile_index(i, rows_ref, cols_ref, live_ref, nb_ref):
        return (0, 0, jnp.minimum(i, nb_ref[0] - 1), 0, 0)

    if mode == "image":
        out_shape = jax.ShapeDtypeStruct((row_blocks, vectors, side), jnp.float32)
        out_spec = pl.BlockSpec((row_blocks, vectors, side), lambda i, *_: (0, 0, 0))
    else:
        out_shape = jax.ShapeDtypeStruct((slots, vectors, 128), jnp.float32)
        out_spec = pl.BlockSpec((group_size, vectors, 128), lambda i, *_: (i, 0, 0))
    grid_spec = pltpu.PrefetchScalarGridSpec(
        num_scalar_prefetch=4,
        grid=(steps,),
        in_specs=[
            pl.BlockSpec((col_blocks, vectors, side), lambda i, *_: (0, 0, 0)),
            pl.BlockSpec((None, None, group_size, side, side), tile_index),
        ],
        out_specs=out_spec,
    )
    return pl.pallas_call(
        functools.partial(tile_kernel, mode),
        grid_spec=grid_spec,
        out_shape=out_shape,
        compiler_params=pltpu.CompilerParams(dimension_semantics=("arbitrary",)),
    )(rows, cols, live, block_count, x_cols, tiles)


def per_device(
    teleport, tiles, tile_rows, tile_cols, tile_counts, dangling, agg_of_block, owner_list
):
    vectors = teleport.shape[0]
    piece_width = teleport.shape[2]
    slots_total = tiles.shape[2]
    tile_side = tiles.shape[4]
    blocks_piece = piece_width // tile_side
    src_count = lax.axis_size("src")
    dst_count = lax.axis_size("dst")
    row_blocks = blocks_piece * src_count
    col_blocks = blocks_piece * dst_count
    page_total = row_blocks * dst_count * tile_side
    agg_count = owner_list.shape[0]
    src_index = lax.axis_index("src")
    dst_index = lax.axis_index("dst")
    own_rows = jnp.clip(tile_rows[0, 0], 0, row_blocks - 1)
    own_cols = jnp.clip(tile_cols[0, 0], 0, col_blocks - 1)
    own_count = tile_counts[0, 0]
    col_global = (
        own_cols // blocks_piece * (blocks_piece * src_count)
        + src_index * blocks_piece
        + own_cols % blocks_piece
    )
    row_global = dst_index * row_blocks + own_rows
    slot_range = jnp.arange(slots_total, dtype=jnp.int32)
    live_mask = ((slot_range < own_count) & (dangling[col_global] == 0)).astype(jnp.int32)
    steps = slots_total // group_size
    block_count = jnp.clip((own_count + group_size - 1) // group_size, 1, steps).reshape(1)
    block_count = block_count.astype(jnp.int32)
    piece_first = dst_index * row_blocks + src_index * blocks_piece
    piece_dangling = lax.dynamic_slice_in_dim(dangling, piece_first, blocks_piece).astype(
        jnp.float32
    )
    piece_agg = lax.dynamic_slice_in_dim(agg_of_block, piece_first, blocks_piece)
    agg_range = jnp.arange(agg_count, dtype=jnp.int32)
    piece_hot = (piece_agg[:, None] == agg_range[None, :]).astype(jnp.float32)
    tele = jnp.transpose(teleport.reshape(vectors, blocks_piece, tile_side), (1, 0, 2))

    def spread_columns(blocks):
        return lax.all_gather(blocks.astype(jnp.bfloat16), "dst", axis=0, tiled=True)

    def reduce_rows(accumulated):
        n = src_count
        if n % 2 == 0 and n > 1:
            half = n // 2
            chunks = accumulated.reshape(half, 2, blocks_piece, vectors, tile_side)
            core = src_index % 2
            keep = lax.dynamic_index_in_dim(chunks, core, 1, keepdims=False)
            give = lax.dynamic_index_in_dim(chunks, 1 - core, 1, keepdims=False)
            got = lax.ppermute(give, "src", [(i, i ^ 1) for i in range(n)])
            part = keep + got
            chip = src_index // 2
            total = lax.dynamic_index_in_dim(part, chip, 0, keepdims=False)
            for shift in range(1, half):
                send = lax.dynamic_index_in_dim(part, (chip + shift) % half, 0, keepdims=False)
                pairs = [(i, ((i // 2 + shift) % half) * 2 + i % 2) for i in range(n)]
                total = total + lax.ppermute(send, "src", pairs)
            return total
        chunks = accumulated.reshape(n, blocks_piece, vectors, tile_side)
        total = lax.dynamic_index_in_dim(chunks, src_index, 0, keepdims=False)
        for shift in range(1, n):
            send = lax.dynamic_index_in_dim(chunks, (src_index + shift) % n, 0, keepdims=False)
            total = total + lax.ppermute(send, "src", [(i, (i + shift) % n) for i in range(n)])
        return total

    def lost_partial(blocks):
        return jnp.sum(blocks * piece_dangling[:, None, None], axis=(0, 2))

    def relaxation(blocks, lost_sum):
        gathered = spread_columns(blocks)
        accumulated = tile_pass(
            "image", gathered, tiles, own_rows, own_cols, live_mask, block_count, row_blocks
        )
        image = reduce_rows(accumulated)
        return (
            damping * (image + (lost_sum / page_total)[None, :, None] * tele)
            + (1.0 - damping) * tele
        )

    tele_sums = jnp.sum(tele, axis=2)
    weight_partial = jnp.einsum("bk,ba->ka", tele_sums, piece_hot, precision=highest)
    start_sums = lax.psum(
        jnp.concatenate([lost_partial(tele)[:, None], weight_partial], axis=1), ("src", "dst")
    )
    lost_zero = start_sums[:, 0]
    weight = start_sums[:, 1:]

    relaxed_one = relaxation(tele, lost_zero)
    lost_one = lax.psum(lost_partial(relaxed_one), ("src", "dst"))
    relaxed_two = relaxation(relaxed_one, lost_one)

    gathered = spread_columns(relaxed_two)
    entries = tile_pass(
        "entries", gathered, tiles, own_rows, own_cols, live_mask, block_count, row_blocks
    )[:, :, 0]
    block_sums = jnp.sum(relaxed_two, axis=2)
    totals_partial = jnp.einsum("bk,ba->ka", block_sums, piece_hot, precision=highest)
    lost_mass_partial = jnp.einsum(
        "bk,ba->ka", block_sums * piece_dangling[:, None], piece_hot, precision=highest
    )
    row_agg = agg_of_block[row_global]
    col_agg = agg_of_block[col_global]
    row_hot = (row_agg[:, None] == agg_range[None, :]).astype(jnp.float32)
    col_hot = (col_agg[:, None] == agg_range[None, :]).astype(jnp.float32)
    inflow_partial = jnp.einsum("tk,ta->ka", entries, row_hot, precision=highest)
    inflow_one, totals, lost_mass = lax.psum(
        jnp.stack([inflow_partial, totals_partial, lost_mass_partial]), ("src", "dst")
    )

    def coarse_sweep(inflow, ratios):
        carried = jnp.sum(lost_mass * ratios, axis=1)
        return (
            damping * (inflow + (carried / page_total)[:, None] * weight)
            + (1.0 - damping) * weight
        )

    level_one = coarse_sweep(inflow_one, jnp.ones((vectors, agg_count), jnp.float32))
    ratios_one = level_one / totals
    ratio_at_tile = jnp.einsum("ka,ta->tk", ratios_one, col_hot, precision=highest)
    inflow_two = lax.psum(
        jnp.einsum("tk,ta->ka", entries * ratio_at_tile, row_hot, precision=highest),
        ("src", "dst"),
    )
    level_two = coarse_sweep(inflow_two, ratios_one)
    ratios_two = level_two / totals
    rescale = jnp.einsum("ka,ba->bk", ratios_two, piece_hot, precision=highest)
    corrected = relaxed_two * rescale[:, :, None]
    lost_two = jnp.sum(lost_mass * ratios_two, axis=1)

    position = lax.axis_index(("src", "dst"))
    owned_count = agg_count // (src_count * dst_count)
    owned = lax.dynamic_slice_in_dim(owner_list, position * owned_count, owned_count)
    owned_hot = (owned[:, None] == agg_range[None, :]).astype(jnp.float32)
    coarse_out = jnp.einsum("ka,qa->kq", level_two, owned_hot, precision=highest)

    relaxed_three = relaxation(corrected, lost_two)
    lost_three = lax.psum(lost_partial(relaxed_three), ("src", "dst"))
    relaxed_four = relaxation(relaxed_three, lost_three)
    fine_out = jnp.transpose(relaxed_four, (1, 0, 2)).reshape(teleport.shape)
    return fine_out, coarse_out


def solution(mesh):
    placed = (
        P(None, "dst", "src"),
        P("dst", "src", None, None, None),
        P("dst", "src", None),
        P("dst", "src", None),
        P("dst", "src"),
        P(),
        P(),
        P(),
    )
    return jax.shard_map(
        per_device,
        mesh=mesh,
        in_specs=placed,
        out_specs=(P(None, "dst", "src"), P(None, ("src", "dst"))),
        check_vma=False,
    )
```

time: 1120 us -> 418 us (0.37)
  blocking collectives: 644 us -> 296 us
  local copies, waits for them, and re-layouts: 244 us -> 11.2 us
  waiting for transfers between devices: 138 us -> 15.8 us
  Pallas kernels: 0 us -> 53.6 us
  other arithmetic: 56.9 us -> 9.53 us
  starting transfers between devices: 0.39 us -> 24.4 us
  between operations: 15.7 us -> 1.74 us
  matrix products: 14.4 us -> 2.18 us
    psum x5, blocking collectives: 471 us -> 242 us  [the longest x1 52.5 us: per_device(): lax.psum(jnp.stack([inflow_partial, totals_partial, lost_mass_partial]),...]
    gather x65 -> x0, local copies, waits for them, and re-layouts: 223 us -> none  [the longest x32 204 us: advance(): picked = jnp.take(tile_set, slot_pick, axis=0)]
    unnamed x10 -> x0, waiting for transfers between devices: 138 us -> none
    all_gather x7 -> x5, blocking collectives: 173 us -> 54.7 us  [spread_columns(): lax.all_gather(blocks.astype(jnp.bfloat16), 'dst', axis=0, tiled=True)]
    pallas_call x0 -> x5, Pallas kernels: none -> 53.6 us  [tile_pass(): pl.pallas_call(functools.partial(tile_kernel, mode), grid_spec=grid_spec,...]
    scatter-add x32 -> x0, other arithmetic: 31 us -> none  [advance(): return accumulated.at[row_pick].add(product.reshape(group_size, flat_width))]
    ppermute x0 -> x16, starting transfers between devices: none -> 24.4 us  [the longest x12 24 us: reduce_rows(): total = total + lax.ppermute(send, 'src', pairs)]
    ppermute x0 -> x16, waiting for transfers between devices: none -> 15.8 us  [the longest x12 14.2 us: reduce_rows(): total = total + lax.ppermute(send, 'src', pairs)]
  transfers between devices with their start and end apart: 5 -> 16, of which waited for: 5 -> 10; matrix products, arithmetic and copies ran while one was open for 1% -> 1% of each run, Pallas kernels for 0% -> 0%
where the time goes in v1:
time: 418 us; the launch traced here: 415 us
  blocking collectives  296 us (71%)
  Pallas kernels  53.6 us (13%)
  starting transfers between devices  24.4 us (6%)
  waiting for transfers between devices  15.8 us (4%)
  local copies, waits for them, and re-layouts  11.2 us (3%)
  other arithmetic  9.53 us (2%)
    all_gather x5, blocking collectives, spread_columns(): lax.all_gather(blocks.astype(jnp.bfloat16), 'dst', axis=0, tiled=True)  54.7 us
    pallas_call x5, Pallas kernels, tile_pass(): pl.pallas_call(functools.partial(tile_kernel, mode), grid_spec=grid_spec,...  53.6 us
    psum x1, blocking collectives, per_device(): lax.psum(jnp.stack([inflow_partial, totals_partial, lost_mass_partial]),...  52.5 us
    psum x1, blocking collectives, per_device(): lost_one = lax.psum(lost_partial(relaxed_one), ('src', 'dst'))  50.8 us
    psum x1, blocking collectives, per_device(): lax.psum(jnp.concatenate([lost_partial(tele)[:, None], weight_partial], a...  50.8 us
    psum x1, blocking collectives, per_device(): lost_three = lax.psum(lost_partial(relaxed_three), ('src', 'dst'))  47.5 us
    psum x1, blocking collectives, per_device(): lax.psum(jnp.einsum('tk,ta->ka', entries * ratio_at_tile, row_hot, precis...  39.9 us
    ppermute x12, starting transfers between devices, reduce_rows(): total = total + lax.ppermute(send, 'src', pairs)  24 us
  transfers between devices with their start and end apart: 16, of which 10 were waited for; matrix products, arithmetic and copies ran while one was open for 1% of the time, Pallas kernels for 0%

profile of v1, /device:TPU:0, one launch (start us, length us, event | category | flops | bytes accessed | tf_op | source)
XLA Modules:
  0.0 414.6 jit_solution(13989759753427796648)
XLA Ops:
  4.3 10.6 %all_gather.15.x_ref = bf16[16,16,256]{2,1,0:T(8,128)(2,1)} all-gather(bf16[4,16,256]{2,1,0:T(8,128)(2,1)S(1)} %copy.58), channel_id=1, replica_groups=mesh['src'=8,'dst'=4] {'dst'}, dimensions={0}, use_global_device_ids=true | all-gather | bytes 163840 | tf_op jit(solution)/shard_map/all_gather | solution.py:117
  14.9 1.6 gather_fusion
  17.1 9.7 %shard_map.95 = f32[32,16,256]{2,1,0:T(8,128)} custom-call(s32[128]{0:T(128)} %get-tuple-element.41.rows_ref, s32[128]{0:T(128)} %get-tuple-element.40.cols_ref, s32[128]{0:T(128)} %and_convert_fusion.live_ref, s32[1]{0:T(128)} %bitcast.5.nb_ref, bf16[16,16,256]{2,1,0:T(8,128)(2,1)} %all_gather.15.x_ref, bf16[1,1,128,256,256]{4,3,2,1,0:T(8,128)(2,1)} %t_ref.9), custom_call_target="tpu_custom_call" | custom-call | tf_op jit(solution)/shard_map/pallas_call | solution.py:69
  28.7 50.8 %psum.35 = f32[16,65]{1,0:T(8,128)S(1)} all-reduce(f32[16,65]{1,0:T(8,128)S(1)} %pad_maximum_fusion.1), channel_id=1, replica_groups=mesh['src'=8,'dst'=4] {'src','dst'}, use_global_device_ids=true, to_apply=%region_2.3 | all-reduce | flops 1040 | bytes 8320 | tf_op jit(solution)/shard_map/psum | solution.py:159
  81.2 1.8 collective-permute-start.2
  83.0 2.1 collective-permute-start.3
  85.2 1.9 collective-permute-done.1
  87.1 1.3 collective-permute-done.2
  88.7 9.8 %all_gather.16.x_ref = bf16[16,16,256]{2,1,0:T(8,128)(2,1)} all-gather(bf16[4,16,256]{2,1,0:T(8,128)(2,1)S(1)} %copy.66), channel_id=1, replica_groups=mesh['src'=8,'dst'=4] {'dst'}, dimensions={0}, use_global_device_ids=true | all-gather | bytes 163840 | tf_op jit(solution)/shard_map/all_gather | solution.py:117
  98.5 9.7 %shard_map.96 = f32[32,16,256]{2,1,0:T(8,128)} custom-call(s32[128]{0:T(128)} %get-tuple-element.41.rows_ref, s32[128]{0:T(128)} %get-tuple-element.40.cols_ref, s32[128]{0:T(128)} %and_convert_fusion.live_ref, s32[1]{0:T(128)} %bitcast.5.nb_ref, bf16[16,16,256]{2,1,0:T(8,128)(2,1)} %all_gather.16.x_ref, bf16[1,1,128,256,256]{4,3,2,1,0:T(8,128)(2,1)} %t_ref.9), custom_call_target="tpu_custom_call" | custom-call | tf_op jit(solution)/shard_map/pallas_call | solution.py:69
  111.7 50.8 %psum.36 = f32[16]{0:T(128)S(1)} all-reduce(f32[16]{0:T(128)S(1)} %get-tuple-element.20), channel_id=1, replica_groups=mesh['src'=8,'dst'=4] {'src','dst'}, use_global_device_ids=true, to_apply=%region_4.5 | all-reduce | flops 16 | bytes 128 | tf_op jit(solution)/shard_map/psum | solution.py:166
  163.8 2.2 collective-permute-start.6
  166.0 1.8 collective-permute-start.7
  167.8 2.3 collective-permute-done.5
  171.7 9.9 %all_gather.17.x_ref = bf16[16,16,256]{2,1,0:T(8,128)(2,1)} all-gather(bf16[4,16,256]{2,1,0:T(8,128)(2,1)S(1)} %copy.73), channel_id=1, replica_groups=mesh['src'=8,'dst'=4] {'dst'}, dimensions={0}, use_global_device_ids=true | all-gather | bytes 163840 | tf_op jit(solution)/shard_map/all_gather | solution.py:117
  181.6 14.6 %shard_map.97 = f32[128,16,128]{2,1,0:T(8,128)} custom-call(s32[128]{0:T(128)} %get-tuple-element.41.rows_ref, s32[128]{0:T(128)} %get-tuple-element.40.cols_ref, s32[128]{0:T(128)} %and_convert_fusion.live_ref, s32[1]{0:T(128)} %bitcast.5.nb_ref, bf16[16,16,256]{2,1,0:T(8,128)(2,1)} %all_gather.17.x_ref, bf16[1,1,128,256,256]{4,3,2,1,0:T(8,128)(2,1)} %t_ref.9), custom_call_target="tpu_custom_call" | custom-call | tf_op jit(solution)/shard_map/pallas_call | solution.py:69
  196.2 1.6 copy.74
  198.1 52.5 %psum.37 = f32[3,16,64]{2,1,0:T(8,128)S(1)} all-reduce(f32[3,16,64]{2,1,0:T(8,128)S(1)} %pad_maximum_fusion), channel_id=1, replica_groups=mesh['src'=8,'dst'=4] {'src','dst'}, use_global_device_ids=true, to_apply=%region_6.7 | all-reduce | flops 3072 | bytes 24576 | tf_op jit(solution)/shard_map/psum | solution.py:183
  251.3 39.9 %psum.38 = f32[16,64]{1,0:T(8,128)S(1)} all-reduce(f32[16,64]{1,0:T(8,128)S(1)} %fusion.22), channel_id=1, replica_groups=mesh['src'=8,'dst'=4] {'src','dst'}, use_global_device_ids=true, to_apply=%region_8.9 | all-reduce | flops 1024 | bytes 8192 | tf_op jit(solution)/shard_map/psum | solution.py:197
  291.7 10.0 %all_gather.18.x_ref = bf16[16,16,256]{2,1,0:T(8,128)(2,1)} all-gather(bf16[4,16,256]{2,1,0:T(8,128)(2,1)S(1)} %copy.76), channel_id=1, replica_groups=mesh['src'=8,'dst'=4] {'dst'}, dimensions={0}, use_global_device_ids=true | all-gather | bytes 163840 | tf_op jit(solution)/shard_map/all_gather | solution.py:117
  301.7 9.9 %shard_map.98 = f32[32,16,256]{2,1,0:T(8,128)} custom-call(s32[128]{0:T(128)} %get-tuple-element.41.rows_ref, s32[128]{0:T(128)} %get-tuple-element.40.cols_ref, s32[128]{0:T(128)} %and_convert_fusion.live_ref, s32[1]{0:T(128)} %bitcast.5.nb_ref, bf16[16,16,256]{2,1,0:T(8,128)(2,1)} %all_gather.18.x_ref, bf16[1,1,128,256,256]{4,3,2,1,0:T(8,128)(2,1)} %t_ref.9), custom_call_target="tpu_custom_call" | custom-call | tf_op jit(solution)/shard_map/pallas_call | solution.py:69
  312.6 1.5 collective-permute-done.8
  315.2 9.6 %collective-permute-start.10 = (f32[4,16,256]{2,0,1:T(4,128)S(1)}, f32[4,16,256]{2,0,1:T(4,128)S(1)}, u32[]{:S(2)}, u32[]{:S(2)}) collective-permute-start(f32[4,16,256]{2,0,1:T(4,128)S(1)} %bitcast.238), channel_id=1, source_target_pairs={{0,16},{4,20},{8,24},{12,28},{16,0},{20,4},{24,8},{28,12},{1,17},{... | collective-permute-start | bytes 196616 | tf_op jit(solution)/shard_map/ppermute | solution.py:134
  325.3 1.7 collective-permute-start.9
  327.0 2.1 collective-permute-done.10
  330.1 1.3 collective-permute-done.9
  331.8 14.4 %all_gather.19.x_ref = bf16[16,16,256]{2,1,0:T(8,128)(2,1)} all-gather(bf16[4,16,256]{2,1,0:T(8,128)(2,1)S(1)} %copy.83), channel_id=1, replica_groups=mesh['src'=8,'dst'=4] {'dst'}, dimensions={0}, use_global_device_ids=true | all-gather | bytes 163840 | tf_op jit(solution)/shard_map/all_gather | solution.py:117
  346.2 9.7 %shard_map.99 = f32[32,16,256]{2,1,0:T(8,128)} custom-call(s32[128]{0:T(128)} %get-tuple-element.41.rows_ref, s32[128]{0:T(128)} %get-tuple-element.40.cols_ref, s32[128]{0:T(128)} %and_convert_fusion.live_ref, s32[1]{0:T(128)} %bitcast.5.nb_ref, bf16[16,16,256]{2,1,0:T(8,128)(2,1)} %all_gather.19.x_ref, bf16[1,1,128,256,256]{4,3,2,1,0:T(8,128)(2,1)} %t_ref.9), custom_call_target="tpu_custom_call" | custom-call | tf_op jit(solution)/shard_map/pallas_call | solution.py:69
  357.8 47.5 %psum.39 = f32[16]{0:T(128)S(1)} all-reduce(f32[16]{0:T(128)S(1)} %get-tuple-element.12), channel_id=1, replica_groups=mesh['src'=8,'dst'=4] {'src','dst'}, use_global_device_ids=true, to_apply=%region_12.13 | all-reduce | flops 16 | bytes 128 | tf_op jit(solution)/shard_map/psum | solution.py:214
  406.5 2.2 collective-permute-start.14
  408.7 1.8 collective-permute-start.15
  410.5 2.3 collective-permute-done.13
  (93 shorter events, 24.1 us)
Async XLA Ops:
  0.6 27.3 %copy-start.1 = (s32[128]{0:T(128)S(1)}, s32[128]{0:T(128)}, u32[]{:S(2)}) copy-start(s32[128]{0:T(128)} %param.13) | copy-start | bytes 1540
  0.6 27.7 %copy-start = (s32[128]{0:T(128)S(1)}, s32[128]{0:T(128)}, u32[]{:S(2)}) copy-start(s32[128]{0:T(128)} %param.14) | copy-start | bytes 1540
  27.8 51.8 %collective-permute-start = (f32[4,4,16,256]{3,2,1,0:T(8,128)S(1)}, f32[4,4,16,256]{3,2,1,0:T(8,128)S(1)}, u32[]{:S(2)}, u32[]{:S(2)}) collective-permute-start(f32[4,4,16,256]{3,2,1,0:T(8,128)S(1)} %dynamic-slice_bitcast_fusion.3), channel_id=1, source_target_pairs={{0,4},{4,0},{8,12},{12,8},{16,20},{20,16},{24,28},{28,24},{1,5},{5... | collective-permute-start | bytes 786440 | tf_op jit(solution)/shard_map/ppermute | solution.py:127
  80.7 6.4 %collective-permute-start.1 = (f32[4,16,256]{2,0,1:T(4,128)S(1)}, f32[4,16,256]{2,0,1:T(4,128)S(1)}, u32[]{:S(2)}, u32[]{:S(2)}) collective-permute-start(f32[4,16,256]{2,0,1:T(4,128)S(1)} %bitcast.241), channel_id=1, source_target_pairs={{0,8},{4,12},{8,16},{12,20},{16,24},{20,28},{24,0},{28,4},{1,9},{5... | collective-permute-start | bytes 196616 | tf_op jit(solution)/shard_map/ppermute | solution.py:134
  81.2 7.2 %collective-permute-start.2 = (f32[4,16,256]{2,0,1:T(4,128)S(1)}, f32[4,16,256]{2,0,1:T(4,128)S(1)}, u32[]{:S(2)}, u32[]{:S(2)}) collective-permute-start(f32[4,16,256]{2,0,1:T(4,128)S(1)} %bitcast.245), channel_id=1, source_target_pairs={{0,16},{4,20},{8,24},{12,28},{16,0},{20,4},{24,8},{28,12},{1,17},{... | collective-permute-start | bytes 196616 | tf_op jit(solution)/shard_map/ppermute | solution.py:134
  83.0 5.4 %collective-permute-start.3 = (f32[4,16,256]{2,0,1:T(4,128)S(1)}, f32[4,16,256]{2,0,1:T(4,128)S(1)}, u32[]{:S(2)}, u32[]{:S(2)}) collective-permute-start(f32[4,16,256]{2,0,1:T(4,128)S(1)} %bitcast.249), channel_id=1, source_target_pairs={{0,24},{4,28},{8,0},{12,4},{16,8},{20,12},{24,16},{28,20},{1,25},{... | collective-permute-start | bytes 196616 | tf_op jit(solution)/shard_map/ppermute | solution.py:134
  109.1 53.4 %collective-permute-start.4 = (f32[4,4,16,256]{3,2,1,0:T(8,128)S(1)}, f32[4,4,16,256]{3,2,1,0:T(8,128)S(1)}, u32[]{:S(2)}, u32[]{:S(2)}) collective-permute-start(f32[4,4,16,256]{3,2,1,0:T(8,128)S(1)} %dynamic-slice_bitcast_fusion.2), channel_id=1, source_target_pairs={{0,4},{4,0},{8,12},{12,8},{16,20},{20,16},{24,28},{28,24},{1,5},{5... | collective-permute-start | bytes 786440 | tf_op jit(solution)/shard_map/ppermute | solution.py:127
  163.6 6.4 %collective-permute-start.5 = (f32[4,16,256]{2,0,1:T(4,128)S(1)}, f32[4,16,256]{2,0,1:T(4,128)S(1)}, u32[]{:S(2)}, u32[]{:S(2)}) collective-permute-start(f32[4,16,256]{2,0,1:T(4,128)S(1)} %bitcast.239), channel_id=1, source_target_pairs={{0,8},{4,12},{8,16},{12,20},{16,24},{20,28},{24,0},{28,4},{1,9},{5... | collective-permute-start | bytes 196616 | tf_op jit(solution)/shard_map/ppermute | solution.py:134
  163.8 7.3 %collective-permute-start.6 = (f32[4,16,256]{2,0,1:T(4,128)S(1)}, f32[4,16,256]{2,0,1:T(4,128)S(1)}, u32[]{:S(2)}, u32[]{:S(2)}) collective-permute-start(f32[4,16,256]{2,0,1:T(4,128)S(1)} %bitcast.243), channel_id=1, source_target_pairs={{0,16},{4,20},{8,24},{12,28},{16,0},{20,4},{24,8},{28,12},{1,17},{... | collective-permute-start | bytes 196616 | tf_op jit(solution)/shard_map/ppermute | solution.py:134
  166.0 5.1 %collective-permute-start.7 = (f32[4,16,256]{2,0,1:T(4,128)S(1)}, f32[4,16,256]{2,0,1:T(4,128)S(1)}, u32[]{:S(2)}, u32[]{:S(2)}) collective-permute-start(f32[4,16,256]{2,0,1:T(4,128)S(1)} %bitcast.247), channel_id=1, source_target_pairs={{0,24},{4,28},{8,0},{12,4},{16,8},{20,12},{24,16},{28,20},{1,25},{... | collective-permute-start | bytes 196616 | tf_op jit(solution)/shard_map/ppermute | solution.py:134
  301.7 55.3 %copy-start.2 = (s32[64]{0:T(128)S(1)}, s32[64]{0:T(128)}, u32[]{:S(2)}) copy-start(s32[64]{0:T(128)} %param.15) | copy-start | bytes 772
  312.5 1.6 collective-permute-start.8
  315.2 13.9 %collective-permute-start.10 = (f32[4,16,256]{2,0,1:T(4,128)S(1)}, f32[4,16,256]{2,0,1:T(4,128)S(1)}, u32[]{:S(2)}, u32[]{:S(2)}) collective-permute-start(f32[4,16,256]{2,0,1:T(4,128)S(1)} %bitcast.238), channel_id=1, source_target_pairs={{0,16},{4,20},{8,24},{12,28},{16,0},{20,4},{24,8},{28,12},{1,17},{... | collective-permute-start | bytes 196616 | tf_op jit(solution)/shard_map/ppermute | solution.py:134
  324.8 5.3 %collective-permute-start.11 = (f32[4,16,256]{2,0,1:T(4,128)S(1)}, f32[4,16,256]{2,0,1:T(4,128)S(1)}, u32[]{:S(2)}, u32[]{:S(2)}) collective-permute-start(f32[4,16,256]{2,0,1:T(4,128)S(1)} %bitcast.242), channel_id=1, source_target_pairs={{0,24},{4,28},{8,0},{12,4},{16,8},{20,12},{24,16},{28,20},{1,25},{... | collective-permute-start | bytes 196616 | tf_op jit(solution)/shard_map/ppermute | solution.py:134
  325.3 6.2 %collective-permute-start.9 = (f32[4,16,256]{2,0,1:T(4,128)S(1)}, f32[4,16,256]{2,0,1:T(4,128)S(1)}, u32[]{:S(2)}, u32[]{:S(2)}) collective-permute-start(f32[4,16,256]{2,0,1:T(4,128)S(1)} %bitcast.246), channel_id=1, source_target_pairs={{0,8},{4,12},{8,16},{12,20},{16,24},{20,28},{24,0},{28,4},{1,9},{5... | collective-permute-start | bytes 196616 | tf_op jit(solution)/shard_map/ppermute | solution.py:134
  356.9 48.4 %collective-permute-start.12 = (f32[4,4,16,256]{3,2,1,0:T(8,128)S(1)}, f32[4,4,16,256]{3,2,1,0:T(8,128)S(1)}, u32[]{:S(2)}, u32[]{:S(2)}) collective-permute-start(f32[4,4,16,256]{3,2,1,0:T(8,128)S(1)} %dynamic-slice_bitcast_fusion), channel_id=1, source_target_pairs={{0,4},{4,0},{8,12},{12,8},{16,20},{20,16},{24,28},{28,24},{1,5},{5... | collective-permute-start | bytes 786440 | tf_op jit(solution)/shard_map/ppermute | solution.py:127
  406.4 6.4 %collective-permute-start.13 = (f32[4,16,256]{2,0,1:T(4,128)S(1)}, f32[4,16,256]{2,0,1:T(4,128)S(1)}, u32[]{:S(2)}, u32[]{:S(2)}) collective-permute-start(f32[4,16,256]{2,0,1:T(4,128)S(1)} %bitcast.240), channel_id=1, source_target_pairs={{0,8},{4,12},{8,16},{12,20},{16,24},{20,28},{24,0},{28,4},{1,9},{5... | collective-permute-start | bytes 196616 | tf_op jit(solution)/shard_map/ppermute | solution.py:134
  406.5 7.3 %collective-permute-start.14 = (f32[4,16,256]{2,0,1:T(4,128)S(1)}, f32[4,16,256]{2,0,1:T(4,128)S(1)}, u32[]{:S(2)}, u32[]{:S(2)}) collective-permute-start(f32[4,16,256]{2,0,1:T(4,128)S(1)} %bitcast.244), channel_id=1, source_target_pairs={{0,16},{4,20},{8,24},{12,28},{16,0},{20,4},{24,8},{28,12},{1,17},{... | collective-permute-start | bytes 196616 | tf_op jit(solution)/shard_map/ppermute | solution.py:134
  408.7 5.1 %collective-permute-start.15 = (f32[4,16,256]{2,0,1:T(4,128)S(1)}, f32[4,16,256]{2,0,1:T(4,128)S(1)}, u32[]{:S(2)}, u32[]{:S(2)}) collective-permute-start(f32[4,16,256]{2,0,1:T(4,128)S(1)} %bitcast.248), channel_id=1, source_target_pairs={{0,24},{4,28},{8,0},{12,4},{16,8},{20,12},{24,16},{28,20},{1,25},{... | collective-permute-start | bytes 196616 | tf_op jit(solution)/shard_map/ppermute | solution.py:134

commit v2 on v1

--- a/solution.py
+++ b/solution.py
@@ -113,10 +113,37 @@
     piece_hot = (piece_agg[:, None] == agg_range[None, :]).astype(jnp.float32)
     tele = jnp.transpose(teleport.reshape(vectors, blocks_piece, tile_side), (1, 0, 2))
 
+    all_axes = ("src", "dst")
+    all_count = src_count * dst_count
+
+    def tree_sum(value, axis, size):
+        if size & (size - 1):
+            return lax.psum(value, axis)
+        shift = 1
+        while shift < size:
+            value = value + lax.ppermute(value, axis, [(i, i ^ shift) for i in range(size)])
+            shift *= 2
+        return value
+
+    exchange = dst_count & (dst_count - 1) == 0
+    if exchange:
+        kernel_cols = (
+            (own_cols // blocks_piece) ^ dst_index
+        ) * blocks_piece + own_cols % blocks_piece
+    else:
+        kernel_cols = own_cols
+
     def spread_columns(blocks):
-        return lax.all_gather(blocks.astype(jnp.bfloat16), "dst", axis=0, tiled=True)
-
-    def reduce_rows(accumulated):
+        rounded = blocks.astype(jnp.bfloat16)
+        if not exchange:
+            return lax.all_gather(rounded, "dst", axis=0, tiled=True)
+        pieces = [rounded] + [
+            lax.ppermute(rounded, "dst", [(i, i ^ v) for i in range(dst_count)])
+            for v in range(1, dst_count)
+        ]
+        return jnp.concatenate(pieces, axis=0)
+
+    def reduce_rows(accumulated, lost):
         n = src_count
         if n % 2 == 0 and n > 1:
             half = n // 2
@@ -124,31 +151,44 @@
             core = src_index % 2
             keep = lax.dynamic_index_in_dim(chunks, core, 1, keepdims=False)
             give = lax.dynamic_index_in_dim(chunks, 1 - core, 1, keepdims=False)
-            got = lax.ppermute(give, "src", [(i, i ^ 1) for i in range(n)])
+            got, got_lost = lax.ppermute((give, lost), "src", [(i, i ^ 1) for i in range(n)])
             part = keep + got
+            lost_part = lost + got_lost
             chip = src_index // 2
             total = lax.dynamic_index_in_dim(part, chip, 0, keepdims=False)
+            lost_total = lost_part
             for shift in range(1, half):
                 send = lax.dynamic_index_in_dim(part, (chip + shift) % half, 0, keepdims=False)
                 pairs = [(i, ((i // 2 + shift) % half) * 2 + i % 2) for i in range(n)]
-                total = total + lax.ppermute(send, "src", pairs)
-            return total
+                got, got_lost = lax.ppermute((send, lost_part), "src", pairs)
+                total = total + got
+                lost_total = lost_total + got_lost
+            return total, lost_total
         chunks = accumulated.reshape(n, blocks_piece, vectors, tile_side)
         total = lax.dynamic_index_in_dim(chunks, src_index, 0, keepdims=False)
+        lost_total = lost
         for shift in range(1, n):
             send = lax.dynamic_index_in_dim(chunks, (src_index + shift) % n, 0, keepdims=False)
-            total = total + lax.ppermute(send, "src", [(i, (i + shift) % n) for i in range(n)])
-        return total
+            pairs = [(i, (i + shift) % n) for i in range(n)]
+            got, got_lost = lax.ppermute((send, lost), "src", pairs)
+            total = total + got
+            lost_total = lost_total + got_lost
+        return total, lost_total
 
     def lost_partial(blocks):
         return jnp.sum(blocks * piece_dangling[:, None, None], axis=(0, 2))
 
-    def relaxation(blocks, lost_sum):
+    def relaxation(blocks, lost_sum=None):
+        if lost_sum is None:
+            lost_dst = tree_sum(lost_partial(blocks), "dst", dst_count)
         gathered = spread_columns(blocks)
         accumulated = tile_pass(
-            "image", gathered, tiles, own_rows, own_cols, live_mask, block_count, row_blocks
+            "image", gathered, tiles, own_rows, kernel_cols, live_mask, block_count, row_blocks
         )
-        image = reduce_rows(accumulated)
+        if lost_sum is None:
+            image, lost_sum = reduce_rows(accumulated, lost_dst)
+        else:
+            image, _ = reduce_rows(accumulated, jnp.zeros((vectors,), jnp.float32))
         return (
             damping * (image + (lost_sum / page_total)[None, :, None] * tele)
             + (1.0 - damping) * tele
@@ -156,19 +196,13 @@
 
     tele_sums = jnp.sum(tele, axis=2)
     weight_partial = jnp.einsum("bk,ba->ka", tele_sums, piece_hot, precision=highest)
-    start_sums = lax.psum(
-        jnp.concatenate([lost_partial(tele)[:, None], weight_partial], axis=1), ("src", "dst")
-    )
-    lost_zero = start_sums[:, 0]
-    weight = start_sums[:, 1:]
-
-    relaxed_one = relaxation(tele, lost_zero)
-    lost_one = lax.psum(lost_partial(relaxed_one), ("src", "dst"))
-    relaxed_two = relaxation(relaxed_one, lost_one)
+
+    relaxed_one = relaxation(tele)
+    relaxed_two = relaxation(relaxed_one)
 
     gathered = spread_columns(relaxed_two)
     entries = tile_pass(
-        "entries", gathered, tiles, own_rows, own_cols, live_mask, block_count, row_blocks
+        "entries", gathered, tiles, own_rows, kernel_cols, live_mask, block_count, row_blocks
     )[:, :, 0]
     block_sums = jnp.sum(relaxed_two, axis=2)
     totals_partial = jnp.einsum("bk,ba->ka", block_sums, piece_hot, precision=highest)
@@ -180,8 +214,10 @@
     row_hot = (row_agg[:, None] == agg_range[None, :]).astype(jnp.float32)
     col_hot = (col_agg[:, None] == agg_range[None, :]).astype(jnp.float32)
     inflow_partial = jnp.einsum("tk,ta->ka", entries, row_hot, precision=highest)
-    inflow_one, totals, lost_mass = lax.psum(
-        jnp.stack([inflow_partial, totals_partial, lost_mass_partial]), ("src", "dst")
+    inflow_one, totals, lost_mass, weight = tree_sum(
+        jnp.stack([inflow_partial, totals_partial, lost_mass_partial, weight_partial]),
+        all_axes,
+        all_count,
     )
 
     def coarse_sweep(inflow, ratios):
@@ -194,9 +230,10 @@
     level_one = coarse_sweep(inflow_one, jnp.ones((vectors, agg_count), jnp.float32))
     ratios_one = level_one / totals
     ratio_at_tile = jnp.einsum("ka,ta->tk", ratios_one, col_hot, precision=highest)
-    inflow_two = lax.psum(
+    inflow_two = tree_sum(
         jnp.einsum("tk,ta->ka", entries * ratio_at_tile, row_hot, precision=highest),
-        ("src", "dst"),
+        all_axes,
+        all_count,
     )
     level_two = coarse_sweep(inflow_two, ratios_one)
     ratios_two = level_two / totals
@@ -204,15 +241,14 @@
     corrected = relaxed_two * rescale[:, :, None]
     lost_two = jnp.sum(lost_mass * ratios_two, axis=1)
 
-    position = lax.axis_index(("src", "dst"))
+    position = lax.axis_index(all_axes)
     owned_count = agg_count // (src_count * dst_count)
     owned = lax.dynamic_slice_in_dim(owner_list, position * owned_count, owned_count)
     owned_hot = (owned[:, None] == agg_range[None, :]).astype(jnp.float32)
     coarse_out = jnp.einsum("ka,qa->kq", level_two, owned_hot, precision=highest)
 
     relaxed_three = relaxation(corrected, lost_two)
-    lost_three = lax.psum(lost_partial(relaxed_three), ("src", "dst"))
-    relaxed_four = relaxation(relaxed_three, lost_three)
+    relaxed_four = relaxation(relaxed_three)
     fine_out = jnp.transpose(relaxed_four, (1, 0, 2)).reshape(teleport.shape)
     return fine_out, coarse_out
 

time: 418 us -> 276 us (0.66)
  blocking collectives: 296 us -> 0 us
  starting transfers between devices: 24.4 us -> 107 us
  waiting for transfers between devices: 15.8 us -> 74.8 us
  Pallas kernels: 53.6 us -> 62.6 us
    psum x5 -> x0, blocking collectives: 242 us -> none  [the longest x1 52.5 us: per_device(): lax.psum(jnp.stack([inflow_partial, totals_partial, lost_mass_partial]),...]
    ppermute x16 -> x59, starting transfers between devices: 24.4 us -> 107 us  [the longest x21 41.9 us: reduce_rows(): got, got_lost = lax.ppermute((send, lost_part), 'src', pairs)]
    ppermute x16 -> x59, waiting for transfers between devices: 15.8 us -> 74.8 us  [the longest x16 37.7 us: tree_sum(): lax.ppermute(value, axis, [(i, i ^ shift) for i in range(size)])]
    all_gather x5 -> x0, blocking collectives: 54.7 us -> none  [spread_columns(): lax.all_gather(blocks.astype(jnp.bfloat16), 'dst', axis=0, tiled=True)]
    pallas_call x5, Pallas kernels: 53.6 us -> 62.6 us  [tile_pass(): pl.pallas_call(functools.partial(tile_kernel, mode), grid_spec=grid_spec,...]
  transfers between devices with their start and end apart: 16 -> 59, of which waited for: 10 -> 36; matrix products, arithmetic and copies ran while one was open for 1% -> 5% of each run, Pallas kernels for 0% -> 0%
where the time goes in v2:
time: 276 us; the launch traced here: 273 us
  starting transfers between devices  107 us (39%)
  waiting for transfers between devices  74.8 us (27%)
  Pallas kernels  62.6 us (23%)
  other arithmetic  13.6 us (5%)
  local copies, waits for them, and re-layouts  10.6 us (4%)
    pallas_call x5, Pallas kernels, tile_pass(): pl.pallas_call(functools.partial(tile_kernel, mode), grid_spec=grid_spec,...  62.6 us
    ppermute x21, starting transfers between devices, reduce_rows(): got, got_lost = lax.ppermute((send, lost_part), 'src', pairs)  41.9 us
    ppermute x16, starting transfers between devices, tree_sum(): lax.ppermute(value, axis, [(i, i ^ shift) for i in range(size)])  38.6 us
    ppermute x16, waiting for transfers between devices, tree_sum(): lax.ppermute(value, axis, [(i, i ^ shift) for i in range(size)])  37.7 us
    ppermute x15, starting transfers between devices, spread_columns(): lax.ppermute(rounded, 'dst', [(i, i ^ v) for i in range(dst_count)])  26.6 us
    ppermute x15, waiting for transfers between devices, spread_columns(): lax.ppermute(rounded, 'dst', [(i, i ^ v) for i in range(dst_count)])  17.1 us
    ppermute x21, waiting for transfers between devices, reduce_rows(): got, got_lost = lax.ppermute((send, lost_part), 'src', pairs)  16.9 us
  transfers between devices with their start and end apart: 59, of which 36 were waited for; matrix products, arithmetic and copies ran while one was open for 5% of the time, Pallas kernels for 0%

profile of v2, /device:TPU:0, one launch (start us, length us, event | category | flops | bytes accessed | tf_op | source)
XLA Modules:
  0.0 272.8 jit_solution(15535255188821496597)
XLA Ops:
  1.7 3.0 %collective-permute-start = (bf16[4,16,256]{2,1,0:T(8,128)(2,1)S(1)}, bf16[4,16,256]{2,1,0:T(8,128)(2,1)S(1)}, u32[]{:S(2)}, u32[]{:S(2)}) collective-permute-start(bf16[4,16,256]{2,1,0:T(8,128)(2,1)S(1)} %bitcast.307), channel_id=1, source_target_pairs={{0,1},{1,0},{2,3},{3,2},{4,5},{5,4},{6,7},{7,6},{8,9},{9,8},{10,11... | collective-permute-start | bytes 98312 | tf_op jit(solution)/shard_map/ppermute | solution.py:141
  12.8 11.7 %shard_map.95 = f32[32,16,256]{2,1,0:T(8,128)} custom-call(s32[128]{0:T(128)} %clamp_bitcast_fusion.rows_ref, s32[128]{0:T(128)} %fusion.52.cols_ref, s32[128]{0:T(128)} %and_convert_fusion.live_ref, s32[1]{0:T(128)} %bitcast.5.nb_ref, bf16[16,16,256]{2,1,0:T(8,128)(2,1)} %pad_maximum_fusion.x_ref, bf16[1,1,128,256,256]{4,3,2,1,0:T(8,128)(2,1)} %t_ref.9), custom_call_target="tpu_custom_call" | custom-call | tf_op jit(solution)/shard_map/pallas_call | solution.py:69
  26.5 2.9 %collective-permute-done.7 = f32[16]{0:T(128)S(1)} collective-permute-done((f32[16]{0:T(128)S(1)}, f32[16]{0:T(128)S(1)}, u32[]{:S(2)}, u32[]{:S(2)}) %collective-permute-start.7) | collective-permute-done | bytes 96 | tf_op jit(solution)/shard_map/ppermute | solution.py:124
  29.4 9.9 %collective-permute-start.8 = (f32[16]{0:T(128)S(1)}, f32[16]{0:T(128)S(1)}, u32[]{:S(2)}, u32[]{:S(2)}) collective-permute-start(f32[16]{0:T(128)S(1)} %add.383), channel_id=1, source_target_pairs={{0,2},{1,3},{2,0},{3,1},{4,6},{5,7},{6,4},{7,5},{8,10},{9,11},{10,... | collective-permute-start | bytes 200 | tf_op jit(solution)/shard_map/ppermute | solution.py:124
  42.0 4.3 %collective-permute-start.11 = (f32[16]{0:T(128)S(1)}, f32[16]{0:T(128)S(1)}, u32[]{:S(2)}, u32[]{:S(2)}) collective-permute-start(f32[16]{0:T(128)S(1)} %add.385), channel_id=1, source_target_pairs={{0,16},{4,20},{8,24},{12,28},{16,0},{20,4},{24,8},{28,12},{1,17},{... | collective-permute-start | bytes 200 | tf_op jit(solution)/shard_map/ppermute | solution.py:163
  46.2 2.9 %collective-permute-start.12 = (f32[16]{0:T(128)S(1)}, f32[16]{0:T(128)S(1)}, u32[]{:S(2)}, u32[]{:S(2)}) collective-permute-start(f32[16]{0:T(128)S(1)} %add.385), channel_id=1, source_target_pairs={{0,24},{4,28},{8,0},{12,4},{16,8},{20,12},{24,16},{28,20},{1,25},{... | collective-permute-start | bytes 200 | tf_op jit(solution)/shard_map/ppermute | solution.py:163
  50.8 3.3 %collective-permute-start.6 = (f32[4,16,256]{2,1,0:T(8,128)S(1)}, f32[4,16,256]{2,1,0:T(8,128)S(1)}, u32[]{:S(2)}, u32[]{:S(2)}) collective-permute-start(f32[4,16,256]{2,1,0:T(8,128)S(1)} %get-tuple-element.26), channel_id=1, source_target_pairs={{0,24},{4,28},{8,0},{12,4},{16,8},{20,12},{24,16},{28,20},{1,25},{... | collective-permute-start | bytes 196616 | tf_op jit(solution)/shard_map/ppermute | solution.py:163
  54.1 2.7 %collective-permute-done.4 = f32[4,16,256]{2,1,0:T(8,128)S(1)} collective-permute-done((f32[4,16,256]{2,1,0:T(8,128)S(1)}, f32[4,16,256]{2,1,0:T(8,128)S(1)}, u32[]{:S(2)}, u32[]{:S(2)}) %collective-permute-start.4) | collective-permute-done | bytes 65568 | tf_op jit(solution)/shard_map/ppermute | solution.py:163
  64.3 2.8 %collective-permute-done.15 = bf16[4,16,256]{2,1,0:T(8,128)(2,1)S(1)} collective-permute-done((bf16[4,16,256]{2,1,0:T(8,128)(2,1)S(1)}, bf16[4,16,256]{2,1,0:T(8,128)(2,1)S(1)}, u32[]{:S(2)}, u32[]{:S(2)}) %collective-permute-start.15) | collective-permute-done | bytes 32800 | tf_op jit(solution)/shard_map/ppermute | solution.py:141
  67.8 11.6 %shard_map.96 = f32[32,16,256]{2,1,0:T(8,128)} custom-call(s32[128]{0:T(128)} %clamp_bitcast_fusion.rows_ref, s32[128]{0:T(128)} %fusion.52.cols_ref, s32[128]{0:T(128)} %and_convert_fusion.live_ref, s32[1]{0:T(128)} %bitcast.5.nb_ref, bf16[16,16,256]{2,1,0:T(8,128)(2,1)} %pad_maximum_fusion.1.x_ref, bf16[1,1,128,256,256]{4,3,2,1,0:T(8,128)(2,1)} %t_ref.9), custom_call_target="tpu_custom_call" | custom-call | tf_op jit(solution)/shard_map/pallas_call | solution.py:69
  80.7 3.3 %collective-permute-done.20 = f32[16]{0:T(128)S(1)} collective-permute-done((f32[16]{0:T(128)S(1)}, f32[16]{0:T(128)S(1)}, u32[]{:S(2)}, u32[]{:S(2)}) %collective-permute-start.20) | collective-permute-done | bytes 96 | tf_op jit(solution)/shard_map/ppermute | solution.py:124
  84.1 4.0 %collective-permute-start.21 = (f32[16]{0:T(128)S(1)}, f32[16]{0:T(128)S(1)}, u32[]{:S(2)}, u32[]{:S(2)}) collective-permute-start(f32[16]{0:T(128)S(1)} %add.395), channel_id=1, source_target_pairs={{0,2},{1,3},{2,0},{3,1},{4,6},{5,7},{6,4},{7,5},{8,10},{9,11},{10,... | collective-permute-start | bytes 200 | tf_op jit(solution)/shard_map/ppermute | solution.py:124
  91.0 6.4 %collective-permute-start.24 = (f32[16]{0:T(128)S(1)}, f32[16]{0:T(128)S(1)}, u32[]{:S(2)}, u32[]{:S(2)}) collective-permute-start(f32[16]{0:T(128)S(1)} %add.397), channel_id=1, source_target_pairs={{0,16},{4,20},{8,24},{12,28},{16,0},{20,4},{24,8},{28,12},{1,17},{... | collective-permute-start | bytes 200 | tf_op jit(solution)/shard_map/ppermute | solution.py:163
  97.3 2.8 %collective-permute-start.25 = (f32[16]{0:T(128)S(1)}, f32[16]{0:T(128)S(1)}, u32[]{:S(2)}, u32[]{:S(2)}) collective-permute-start(f32[16]{0:T(128)S(1)} %add.397), channel_id=1, source_target_pairs={{0,24},{4,28},{8,0},{12,4},{16,8},{20,12},{24,16},{28,20},{1,25},{... | collective-permute-start | bytes 200 | tf_op jit(solution)/shard_map/ppermute | solution.py:163
  101.9 3.3 %collective-permute-start.19 = (f32[4,16,256]{2,1,0:T(8,128)S(1)}, f32[4,16,256]{2,1,0:T(8,128)S(1)}, u32[]{:S(2)}, u32[]{:S(2)}) collective-permute-start(f32[4,16,256]{2,1,0:T(8,128)S(1)} %get-tuple-element.23), channel_id=1, source_target_pairs={{0,24},{4,28},{8,0},{12,4},{16,8},{20,12},{24,16},{28,20},{1,25},{... | collective-permute-start | bytes 196616 | tf_op jit(solution)/shard_map/ppermute | solution.py:163
  105.1 3.0 %collective-permute-done.17 = f32[4,16,256]{2,1,0:T(8,128)S(1)} collective-permute-done((f32[4,16,256]{2,1,0:T(8,128)S(1)}, f32[4,16,256]{2,1,0:T(8,128)S(1)}, u32[]{:S(2)}, u32[]{:S(2)}) %collective-permute-start.17) | collective-permute-done | bytes 65568 | tf_op jit(solution)/shard_map/ppermute | solution.py:163
  118.0 16.1 %shard_map.97 = f32[128,16,128]{2,1,0:T(8,128)} custom-call(s32[128]{0:T(128)} %clamp_bitcast_fusion.rows_ref, s32[128]{0:T(128)} %fusion.52.cols_ref, s32[128]{0:T(128)} %and_convert_fusion.live_ref, s32[1]{0:T(128)} %bitcast.5.nb_ref, bf16[16,16,256]{2,1,0:T(8,128)(2,1)} %pad_maximum_fusion.2.x_ref, bf16[1,1,128,256,256]{4,3,2,1,0:T(8,128)(2,1)} %t_ref.9), custom_call_target="tpu_custom_call" | custom-call | tf_op jit(solution)/shard_map/pallas_call | solution.py:69
  136.1 3.9 %collective-permute-done.29 = f32[4,16,64]{2,1,0:T(8,128)S(1)} collective-permute-done((f32[4,16,64]{2,1,0:T(8,128)S(1)}, f32[4,16,64]{2,1,0:T(8,128)S(1)}, u32[]{:S(2)}, u32[]{:S(2)}) %collective-permute-start.29) | collective-permute-done | bytes 16416 | tf_op jit(solution)/shard_map/ppermute | solution.py:124
  140.9 3.0 %collective-permute-done.30 = f32[4,16,64]{2,1,0:T(8,128)S(1)} collective-permute-done((f32[4,16,64]{2,1,0:T(8,128)S(1)}, f32[4,16,64]{2,1,0:T(8,128)S(1)}, u32[]{:S(2)}, u32[]{:S(2)}) %collective-permute-start.30) | collective-permute-done | bytes 16416 | tf_op jit(solution)/shard_map/ppermute | solution.py:124
  147.0 3.9 %collective-permute-done.32 = f32[4,16,64]{2,1,0:T(8,128)S(1)} collective-permute-done((f32[4,16,64]{2,1,0:T(8,128)S(1)}, f32[4,16,64]{2,1,0:T(8,128)S(1)}, u32[]{:S(2)}, u32[]{:S(2)}) %collective-permute-start.32) | collective-permute-done | bytes 16416 | tf_op jit(solution)/shard_map/ppermute | solution.py:124
  150.9 10.0 %collective-permute-start.33 = (f32[4,16,64]{2,1,0:T(8,128)S(1)}, f32[4,16,64]{2,1,0:T(8,128)S(1)}, u32[]{:S(2)}, u32[]{:S(2)}) collective-permute-start(f32[4,16,64]{2,1,0:T(8,128)S(1)} %add.410), channel_id=1, source_target_pairs={{0,16},{1,17},{2,18},{3,19},{4,20},{5,21},{6,22},{7,23},{8,24},{9,... | collective-permute-start | bytes 49160 | tf_op jit(solution)/shard_map/ppermute | solution.py:124
  167.8 3.1 %collective-permute-done.35 = f32[16,64]{1,0:T(8,128)S(1)} collective-permute-done((f32[16,64]{1,0:T(8,128)S(1)}, f32[16,64]{1,0:T(8,128)S(1)}, u32[]{:S(2)}, u32[]{:S(2)}) %collective-permute-start.35) | collective-permute-done | bytes 4128 | tf_op jit(solution)/shard_map/ppermute | solution.py:124
  172.1 3.6 %collective-permute-done.37 = f32[16,64]{1,0:T(8,128)S(1)} collective-permute-done((f32[16,64]{1,0:T(8,128)S(1)}, f32[16,64]{1,0:T(8,128)S(1)}, u32[]{:S(2)}, u32[]{:S(2)}) %collective-permute-start.37) | collective-permute-done | bytes 4128 | tf_op jit(solution)/shard_map/ppermute | solution.py:124
  175.7 2.9 %collective-permute-start.38 = (f32[16,64]{1,0:T(8,128)S(1)}, f32[16,64]{1,0:T(8,128)S(1)}, u32[]{:S(2)}, u32[]{:S(2)}) collective-permute-start(f32[16,64]{1,0:T(8,128)S(1)} %add.417), channel_id=1, source_target_pairs={{0,16},{1,17},{2,18},{3,19},{4,20},{5,21},{6,22},{7,23},{8,24},{9,... | collective-permute-start | bytes 12296 | tf_op jit(solution)/shard_map/ppermute | solution.py:124
  188.9 11.7 %shard_map.98 = f32[32,16,256]{2,1,0:T(8,128)} custom-call(s32[128]{0:T(128)} %clamp_bitcast_fusion.rows_ref, s32[128]{0:T(128)} %fusion.52.cols_ref, s32[128]{0:T(128)} %and_convert_fusion.live_ref, s32[1]{0:T(128)} %bitcast.5.nb_ref, bf16[16,16,256]{2,1,0:T(8,128)(2,1)} %pad_maximum_fusion.3.x_ref, bf16[1,1,128,256,256]{4,3,2,1,0:T(8,128)(2,1)} %t_ref.9), custom_call_target="tpu_custom_call" | custom-call | tf_op jit(solution)/shard_map/pallas_call | solution.py:69
  213.1 8.9 %collective-permute-start.46 = (bf16[4,16,256]{2,1,0:T(8,128)(2,1)S(1)}, bf16[4,16,256]{2,1,0:T(8,128)(2,1)S(1)}, u32[]{:S(2)}, u32[]{:S(2)}) collective-permute-start(bf16[4,16,256]{2,1,0:T(8,128)(2,1)S(1)} %get-tuple-element.7), channel_id=1, source_target_pairs={{0,1},{1,0},{2,3},{3,2},{4,5},{5,4},{6,7},{7,6},{8,9},{9,8},{10,11... | collective-permute-start | bytes 98312 | tf_op jit(solution)/shard_map/ppermute | solution.py:141
  229.3 11.6 %shard_map.99 = f32[32,16,256]{2,1,0:T(8,128)} custom-call(s32[128]{0:T(128)} %clamp_bitcast_fusion.rows_ref, s32[128]{0:T(128)} %fusion.52.cols_ref, s32[128]{0:T(128)} %and_convert_fusion.live_ref, s32[1]{0:T(128)} %bitcast.5.nb_ref, bf16[16,16,256]{2,1,0:T(8,128)(2,1)} %pad_maximum_fusion.4.x_ref, bf16[1,1,128,256,256]{4,3,2,1,0:T(8,128)(2,1)} %t_ref.9), custom_call_target="tpu_custom_call" | custom-call | tf_op jit(solution)/shard_map/pallas_call | solution.py:69
  242.0 3.5 %collective-permute-done.53 = f32[16]{0:T(128)S(1)} collective-permute-done((f32[16]{0:T(128)S(1)}, f32[16]{0:T(128)S(1)}, u32[]{:S(2)}, u32[]{:S(2)}) %collective-permute-start.53) | collective-permute-done | bytes 96 | tf_op jit(solution)/shard_map/ppermute | solution.py:124
  245.5 5.2 %collective-permute-start.54 = (f32[16]{0:T(128)S(1)}, f32[16]{0:T(128)S(1)}, u32[]{:S(2)}, u32[]{:S(2)}) collective-permute-start(f32[16]{0:T(128)S(1)} %add.431), channel_id=1, source_target_pairs={{0,2},{1,3},{2,0},{3,1},{4,6},{5,7},{6,4},{7,5},{8,10},{9,11},{10,... | collective-permute-start | bytes 200 | tf_op jit(solution)/shard_map/ppermute | solution.py:124
  253.4 6.6 %collective-permute-start.57 = (f32[16]{0:T(128)S(1)}, f32[16]{0:T(128)S(1)}, u32[]{:S(2)}, u32[]{:S(2)}) collective-permute-start(f32[16]{0:T(128)S(1)} %add.433), channel_id=1, source_target_pairs={{0,16},{4,20},{8,24},{12,28},{16,0},{20,4},{24,8},{28,12},{1,17},{... | collective-permute-start | bytes 200 | tf_op jit(solution)/shard_map/ppermute | solution.py:163
  260.0 2.9 %collective-permute-start.58 = (f32[16]{0:T(128)S(1)}, f32[16]{0:T(128)S(1)}, u32[]{:S(2)}, u32[]{:S(2)}) collective-permute-start(f32[16]{0:T(128)S(1)} %add.433), channel_id=1, source_target_pairs={{0,24},{4,28},{8,0},{12,4},{16,8},{20,12},{24,16},{28,20},{1,25},{... | collective-permute-start | bytes 200 | tf_op jit(solution)/shard_map/ppermute | solution.py:163
  264.6 3.3 %collective-permute-start.52 = (f32[4,16,256]{2,1,0:T(8,128)S(1)}, f32[4,16,256]{2,1,0:T(8,128)S(1)}, u32[]{:S(2)}, u32[]{:S(2)}) collective-permute-start(f32[4,16,256]{2,1,0:T(8,128)S(1)} %get-tuple-element.17), channel_id=1, source_target_pairs={{0,24},{4,28},{8,0},{12,4},{16,8},{20,12},{24,16},{28,20},{1,25},{... | collective-permute-start | bytes 196616 | tf_op jit(solution)/shard_map/ppermute | solution.py:163
  (174 shorter events, 93.0 us)
Async XLA Ops:
  1.7 10.4 %collective-permute-start = (bf16[4,16,256]{2,1,0:T(8,128)(2,1)S(1)}, bf16[4,16,256]{2,1,0:T(8,128)(2,1)S(1)}, u32[]{:S(2)}, u32[]{:S(2)}) collective-permute-start(bf16[4,16,256]{2,1,0:T(8,128)(2,1)S(1)} %bitcast.307), channel_id=1, source_target_pairs={{0,1},{1,0},{2,3},{3,2},{4,5},{5,4},{6,7},{7,6},{8,9},{9,8},{10,11... | collective-permute-start | bytes 98312 | tf_op jit(solution)/shard_map/ppermute | solution.py:141
  4.7 7.4 %collective-permute-start.1 = (bf16[4,16,256]{2,1,0:T(8,128)(2,1)S(1)}, bf16[4,16,256]{2,1,0:T(8,128)(2,1)S(1)}, u32[]{:S(2)}, u32[]{:S(2)}) collective-permute-start(bf16[4,16,256]{2,1,0:T(8,128)(2,1)S(1)} %bitcast.308), channel_id=1, source_target_pairs={{0,2},{1,3},{2,0},{3,1},{4,6},{5,7},{6,4},{7,5},{8,10},{9,11},{10,... | collective-permute-start | bytes 98312 | tf_op jit(solution)/shard_map/ppermute | solution.py:141
  6.2 5.9 %collective-permute-start.2 = (bf16[4,16,256]{2,1,0:T(8,128)(2,1)S(1)}, bf16[4,16,256]{2,1,0:T(8,128)(2,1)S(1)}, u32[]{:S(2)}, u32[]{:S(2)}) collective-permute-start(bf16[4,16,256]{2,1,0:T(8,128)(2,1)S(1)} %bitcast.309), channel_id=1, source_target_pairs={{0,3},{1,2},{2,1},{3,0},{4,7},{5,6},{6,5},{7,4},{8,11},{9,10},{10,... | collective-permute-start | bytes 98312 | tf_op jit(solution)/shard_map/ppermute | solution.py:141
  25.4 23.7 %collective-permute-start.3 = (f32[4,4,16,256]{3,2,1,0:T(8,128)S(1)}, f32[4,4,16,256]{3,2,1,0:T(8,128)S(1)}, u32[]{:S(2)}, u32[]{:S(2)}) collective-permute-start(f32[4,4,16,256]{3,2,1,0:T(8,128)S(1)} %dynamic-slice_bitcast_fusion.3), channel_id=1, source_target_pairs={{0,4},{4,0},{8,12},{12,8},{16,20},{20,16},{24,28},{28,24},{1,5},{5... | collective-permute-start | bytes 786440 | tf_op jit(solution)/shard_map/ppermute | solution.py:154
  29.4 11.4 %collective-permute-start.8 = (f32[16]{0:T(128)S(1)}, f32[16]{0:T(128)S(1)}, u32[]{:S(2)}, u32[]{:S(2)}) collective-permute-start(f32[16]{0:T(128)S(1)} %add.383), channel_id=1, source_target_pairs={{0,2},{1,3},{2,0},{3,1},{4,6},{5,7},{6,4},{7,5},{8,10},{9,11},{10,... | collective-permute-start | bytes 200 | tf_op jit(solution)/shard_map/ppermute | solution.py:124
  42.0 8.8 %collective-permute-start.10 = (f32[16]{0:T(128)S(1)}, f32[16]{0:T(128)S(1)}, u32[]{:S(2)}, u32[]{:S(2)}) collective-permute-start(f32[16]{0:T(128)S(1)} %add.385), channel_id=1, source_target_pairs={{0,8},{4,12},{8,16},{12,20},{16,24},{20,28},{24,0},{28,4},{1,9},{5... | collective-permute-start | bytes 200 | tf_op jit(solution)/shard_map/ppermute | solution.py:163
  42.0 12.1 %collective-permute-start.11 = (f32[16]{0:T(128)S(1)}, f32[16]{0:T(128)S(1)}, u32[]{:S(2)}, u32[]{:S(2)}) collective-permute-start(f32[16]{0:T(128)S(1)} %add.385), channel_id=1, source_target_pairs={{0,16},{4,20},{8,24},{12,28},{16,0},{20,4},{24,8},{28,12},{1,17},{... | collective-permute-start | bytes 200 | tf_op jit(solution)/shard_map/ppermute | solution.py:163
  46.2 7.8 %collective-permute-start.12 = (f32[16]{0:T(128)S(1)}, f32[16]{0:T(128)S(1)}, u32[]{:S(2)}, u32[]{:S(2)}) collective-permute-start(f32[16]{0:T(128)S(1)} %add.385), channel_id=1, source_target_pairs={{0,24},{4,28},{8,0},{12,4},{16,8},{20,12},{24,16},{28,20},{1,25},{... | collective-permute-start | bytes 200 | tf_op jit(solution)/shard_map/ppermute | solution.py:163
  50.2 6.6 %collective-permute-start.4 = (f32[4,16,256]{2,1,0:T(8,128)S(1)}, f32[4,16,256]{2,1,0:T(8,128)S(1)}, u32[]{:S(2)}, u32[]{:S(2)}) collective-permute-start(f32[4,16,256]{2,1,0:T(8,128)S(1)} %get-tuple-element.25), channel_id=1, source_target_pairs={{0,8},{4,12},{8,16},{12,20},{16,24},{20,28},{24,0},{28,4},{1,9},{5... | collective-permute-start | bytes 196616 | tf_op jit(solution)/shard_map/ppermute | solution.py:163
  50.3 7.9 %collective-permute-start.5 = (f32[4,16,256]{2,1,0:T(8,128)S(1)}, f32[4,16,256]{2,1,0:T(8,128)S(1)}, u32[]{:S(2)}, u32[]{:S(2)}) collective-permute-start(f32[4,16,256]{2,1,0:T(8,128)S(1)} %get-tuple-element.27), channel_id=1, source_target_pairs={{0,16},{4,20},{8,24},{12,28},{16,0},{20,4},{24,8},{28,12},{1,17},{... | collective-permute-start | bytes 196616 | tf_op jit(solution)/shard_map/ppermute | solution.py:163
  50.8 7.3 %collective-permute-start.6 = (f32[4,16,256]{2,1,0:T(8,128)S(1)}, f32[4,16,256]{2,1,0:T(8,128)S(1)}, u32[]{:S(2)}, u32[]{:S(2)}) collective-permute-start(f32[4,16,256]{2,1,0:T(8,128)S(1)} %get-tuple-element.26), channel_id=1, source_target_pairs={{0,24},{4,28},{8,0},{12,4},{16,8},{20,12},{24,16},{28,20},{1,25},{... | collective-permute-start | bytes 196616 | tf_op jit(solution)/shard_map/ppermute | solution.py:163
  80.4 19.8 %collective-permute-start.16 = (f32[4,4,16,256]{3,2,1,0:T(8,128)S(1)}, f32[4,4,16,256]{3,2,1,0:T(8,128)S(1)}, u32[]{:S(2)}, u32[]{:S(2)}) collective-permute-start(f32[4,4,16,256]{3,2,1,0:T(8,128)S(1)} %dynamic-slice_bitcast_fusion.2), channel_id=1, source_target_pairs={{0,4},{4,0},{8,12},{12,8},{16,20},{20,16},{24,28},{28,24},{1,5},{5... | collective-permute-start | bytes 786440 | tf_op jit(solution)/shard_map/ppermute | solution.py:154
  84.1 5.5 %collective-permute-start.21 = (f32[16]{0:T(128)S(1)}, f32[16]{0:T(128)S(1)}, u32[]{:S(2)}, u32[]{:S(2)}) collective-permute-start(f32[16]{0:T(128)S(1)} %add.395), channel_id=1, source_target_pairs={{0,2},{1,3},{2,0},{3,1},{4,6},{5,7},{6,4},{7,5},{8,10},{9,11},{10,... | collective-permute-start | bytes 200 | tf_op jit(solution)/shard_map/ppermute | solution.py:124
  90.9 11.0 %collective-permute-start.23 = (f32[16]{0:T(128)S(1)}, f32[16]{0:T(128)S(1)}, u32[]{:S(2)}, u32[]{:S(2)}) collective-permute-start(f32[16]{0:T(128)S(1)} %add.397), channel_id=1, source_target_pairs={{0,8},{4,12},{8,16},{12,20},{16,24},{20,28},{24,0},{28,4},{1,9},{5... | collective-permute-start | bytes 200 | tf_op jit(solution)/shard_map/ppermute | solution.py:163
  91.0 14.2 %collective-permute-start.24 = (f32[16]{0:T(128)S(1)}, f32[16]{0:T(128)S(1)}, u32[]{:S(2)}, u32[]{:S(2)}) collective-permute-start(f32[16]{0:T(128)S(1)} %add.397), channel_id=1, source_target_pairs={{0,16},{4,20},{8,24},{12,28},{16,0},{20,4},{24,8},{28,12},{1,17},{... | collective-permute-start | bytes 200 | tf_op jit(solution)/shard_map/ppermute | solution.py:163
  97.3 7.8 %collective-permute-start.25 = (f32[16]{0:T(128)S(1)}, f32[16]{0:T(128)S(1)}, u32[]{:S(2)}, u32[]{:S(2)}) collective-permute-start(f32[16]{0:T(128)S(1)} %add.397), channel_id=1, source_target_pairs={{0,24},{4,28},{8,0},{12,4},{16,8},{20,12},{24,16},{28,20},{1,25},{... | collective-permute-start | bytes 200 | tf_op jit(solution)/shard_map/ppermute | solution.py:163
  101.2 6.9 %collective-permute-start.17 = (f32[4,16,256]{2,1,0:T(8,128)S(1)}, f32[4,16,256]{2,1,0:T(8,128)S(1)}, u32[]{:S(2)}, u32[]{:S(2)}) collective-permute-start(f32[4,16,256]{2,1,0:T(8,128)S(1)} %get-tuple-element.22), channel_id=1, source_target_pairs={{0,8},{4,12},{8,16},{12,20},{16,24},{20,28},{24,0},{28,4},{1,9},{5... | collective-permute-start | bytes 196616 | tf_op jit(solution)/shard_map/ppermute | solution.py:163
  101.3 8.2 %collective-permute-start.18 = (f32[4,16,256]{2,1,0:T(8,128)S(1)}, f32[4,16,256]{2,1,0:T(8,128)S(1)}, u32[]{:S(2)}, u32[]{:S(2)}) collective-permute-start(f32[4,16,256]{2,1,0:T(8,128)S(1)} %get-tuple-element.24), channel_id=1, source_target_pairs={{0,16},{4,20},{8,24},{12,28},{16,0},{20,4},{24,8},{28,12},{1,17},{... | collective-permute-start | bytes 196616 | tf_op jit(solution)/shard_map/ppermute | solution.py:163
  101.9 7.6 %collective-permute-start.19 = (f32[4,16,256]{2,1,0:T(8,128)S(1)}, f32[4,16,256]{2,1,0:T(8,128)S(1)}, u32[]{:S(2)}, u32[]{:S(2)}) collective-permute-start(f32[4,16,256]{2,1,0:T(8,128)S(1)} %get-tuple-element.23), channel_id=1, source_target_pairs={{0,24},{4,28},{8,0},{12,4},{16,8},{20,12},{24,16},{28,20},{1,25},{... | collective-permute-start | bytes 196616 | tf_op jit(solution)/shard_map/ppermute | solution.py:163
  150.9 11.9 %collective-permute-start.33 = (f32[4,16,64]{2,1,0:T(8,128)S(1)}, f32[4,16,64]{2,1,0:T(8,128)S(1)}, u32[]{:S(2)}, u32[]{:S(2)}) collective-permute-start(f32[4,16,64]{2,1,0:T(8,128)S(1)} %add.410), channel_id=1, source_target_pairs={{0,16},{1,17},{2,18},{3,19},{4,20},{5,21},{6,22},{7,23},{8,24},{9,... | collective-permute-start | bytes 49160 | tf_op jit(solution)/shard_map/ppermute | solution.py:124
  204.2 6.8 %collective-permute-start.43 = (f32[4,16,256]{2,1,0:T(8,128)S(1)}, f32[4,16,256]{2,1,0:T(8,128)S(1)}, u32[]{:S(2)}, u32[]{:S(2)}) collective-permute-start(f32[4,16,256]{2,1,0:T(8,128)S(1)} %get-tuple-element.19), channel_id=1, source_target_pairs={{0,8},{4,12},{8,16},{12,20},{16,24},{20,28},{24,0},{28,4},{1,9},{5... | collective-permute-start | bytes 196616 | tf_op jit(solution)/shard_map/ppermute | solution.py:163
  204.2 8.6 %collective-permute-start.44 = (f32[4,16,256]{2,1,0:T(8,128)S(1)}, f32[4,16,256]{2,1,0:T(8,128)S(1)}, u32[]{:S(2)}, u32[]{:S(2)}) collective-permute-start(f32[4,16,256]{2,1,0:T(8,128)S(1)} %get-tuple-element.21), channel_id=1, source_target_pairs={{0,16},{4,20},{8,24},{12,28},{16,0},{20,4},{24,8},{28,12},{1,17},{... | collective-permute-start | bytes 196616 | tf_op jit(solution)/shard_map/ppermute | solution.py:163
  207.0 5.9 %collective-permute-start.45 = (f32[4,16,256]{2,1,0:T(8,128)S(1)}, f32[4,16,256]{2,1,0:T(8,128)S(1)}, u32[]{:S(2)}, u32[]{:S(2)}) collective-permute-start(f32[4,16,256]{2,1,0:T(8,128)S(1)} %get-tuple-element.20), channel_id=1, source_target_pairs={{0,24},{4,28},{8,0},{12,4},{16,8},{20,12},{24,16},{28,20},{1,25},{... | collective-permute-start | bytes 196616 | tf_op jit(solution)/shard_map/ppermute | solution.py:163
  213.1 10.8 %collective-permute-start.46 = (bf16[4,16,256]{2,1,0:T(8,128)(2,1)S(1)}, bf16[4,16,256]{2,1,0:T(8,128)(2,1)S(1)}, u32[]{:S(2)}, u32[]{:S(2)}) collective-permute-start(bf16[4,16,256]{2,1,0:T(8,128)(2,1)S(1)} %get-tuple-element.7), channel_id=1, source_target_pairs={{0,1},{1,0},{2,3},{3,2},{4,5},{5,4},{6,7},{7,6},{8,9},{9,8},{10,11... | collective-permute-start | bytes 98312 | tf_op jit(solution)/shard_map/ppermute | solution.py:141
  241.8 21.1 %collective-permute-start.49 = (f32[4,4,16,256]{3,2,1,0:T(8,128)S(1)}, f32[4,4,16,256]{3,2,1,0:T(8,128)S(1)}, u32[]{:S(2)}, u32[]{:S(2)}) collective-permute-start(f32[4,4,16,256]{3,2,1,0:T(8,128)S(1)} %dynamic-slice_bitcast_fusion), channel_id=1, source_target_pairs={{0,4},{4,0},{8,12},{12,8},{16,20},{20,16},{24,28},{28,24},{1,5},{5... | collective-permute-start | bytes 786440 | tf_op jit(solution)/shard_map/ppermute | solution.py:154
  245.5 6.8 %collective-permute-start.54 = (f32[16]{0:T(128)S(1)}, f32[16]{0:T(128)S(1)}, u32[]{:S(2)}, u32[]{:S(2)}) collective-permute-start(f32[16]{0:T(128)S(1)} %add.431), channel_id=1, source_target_pairs={{0,2},{1,3},{2,0},{3,1},{4,6},{5,7},{6,4},{7,5},{8,10},{9,11},{10,... | collective-permute-start | bytes 200 | tf_op jit(solution)/shard_map/ppermute | solution.py:124
  253.4 11.2 %collective-permute-start.56 = (f32[16]{0:T(128)S(1)}, f32[16]{0:T(128)S(1)}, u32[]{:S(2)}, u32[]{:S(2)}) collective-permute-start(f32[16]{0:T(128)S(1)} %add.433), channel_id=1, source_target_pairs={{0,8},{4,12},{8,16},{12,20},{16,24},{20,28},{24,0},{28,4},{1,9},{5... | collective-permute-start | bytes 200 | tf_op jit(solution)/shard_map/ppermute | solution.py:163
  253.4 14.4 %collective-permute-start.57 = (f32[16]{0:T(128)S(1)}, f32[16]{0:T(128)S(1)}, u32[]{:S(2)}, u32[]{:S(2)}) collective-permute-start(f32[16]{0:T(128)S(1)} %add.433), channel_id=1, source_target_pairs={{0,16},{4,20},{8,24},{12,28},{16,0},{20,4},{24,8},{28,12},{1,17},{... | collective-permute-start | bytes 200 | tf_op jit(solution)/shard_map/ppermute | solution.py:163
  260.0 7.8 %collective-permute-start.58 = (f32[16]{0:T(128)S(1)}, f32[16]{0:T(128)S(1)}, u32[]{:S(2)}, u32[]{:S(2)}) collective-permute-start(f32[16]{0:T(128)S(1)} %add.433), channel_id=1, source_target_pairs={{0,24},{4,28},{8,0},{12,4},{16,8},{20,12},{24,16},{28,20},{1,25},{... | collective-permute-start | bytes 200 | tf_op jit(solution)/shard_map/ppermute | solution.py:163
  264.0 6.6 %collective-permute-start.50 = (f32[4,16,256]{2,1,0:T(8,128)S(1)}, f32[4,16,256]{2,1,0:T(8,128)S(1)}, u32[]{:S(2)}, u32[]{:S(2)}) collective-permute-start(f32[4,16,256]{2,1,0:T(8,128)S(1)} %get-tuple-element.16), channel_id=1, source_target_pairs={{0,8},{4,12},{8,16},{12,20},{16,24},{20,28},{24,0},{28,4},{1,9},{5... | collective-permute-start | bytes 196616 | tf_op jit(solution)/shard_map/ppermute | solution.py:163
  264.1 7.9 %collective-permute-start.51 = (f32[4,16,256]{2,1,0:T(8,128)S(1)}, f32[4,16,256]{2,1,0:T(8,128)S(1)}, u32[]{:S(2)}, u32[]{:S(2)}) collective-permute-start(f32[4,16,256]{2,1,0:T(8,128)S(1)} %get-tuple-element.18), channel_id=1, source_target_pairs={{0,16},{4,20},{8,24},{12,28},{16,0},{20,4},{24,8},{28,12},{1,17},{... | collective-permute-start | bytes 196616 | tf_op jit(solution)/shard_map/ppermute | solution.py:163
  264.6 7.3 %collective-permute-start.52 = (f32[4,16,256]{2,1,0:T(8,128)S(1)}, f32[4,16,256]{2,1,0:T(8,128)S(1)}, u32[]{:S(2)}, u32[]{:S(2)}) collective-permute-start(f32[4,16,256]{2,1,0:T(8,128)S(1)} %get-tuple-element.17), channel_id=1, source_target_pairs={{0,24},{4,28},{8,0},{12,4},{16,8},{20,12},{24,16},{28,20},{1,25},{... | collective-permute-start | bytes 196616 | tf_op jit(solution)/shard_map/ppermute | solution.py:163
  (30 other events, 249.6 us)
